TPU v7x, 256 devices: a whole 4x4x8 slice. The times are simulated.
256 devices in a mesh: dp: 16 (over z, core), expert: 16 (over x, y).
Axes of the slice: x: 4, y: 4, z: 8, core: 2. Of those that a mesh axis runs over, the one named last changes fastest.
Arguments:
- tokens: bfloat16 [32768, 2048], P(('dp', 'expert')), may hold values from -24 to 24
- cotangent: bfloat16 [32768, 2048], P(('dp', 'expert')), may hold values from -6 to 6
- expert_ids: int32 [32768, 2], P(('dp', 'expert')), may hold values from 0 to 15, all different within a row; in each aligned block of 128 rows (0 to 127, 128 to 255, ...) at most 24 rows name the same one
- placed: int32 [16], replicated, may hold values from 0 to 15, as said below
- router_weight: bfloat16 [2048, 16], replicated, may hold values from -0.125 to 0.125
- gate_weight: bfloat16 [16, 2048, 768], P('expert', 'dp'), may hold values from -0.125 to 0.125
- up_weight: bfloat16 [16, 2048, 768], P('expert', 'dp'), may hold values from -0.125 to 0.125
- down_weight: bfloat16 [16, 2048, 768], P('expert', 'dp'), may hold values from -0.21875 to 0.21875
Outputs:
- mixed: bfloat16 [32768, 2048], P(('dp', 'expert'))
- token_grad: bfloat16 [32768, 2048], P(('dp', 'expert'))
- gate_grad: bfloat16 [16, 2048, 768], P('expert', 'dp')
- up_grad: bfloat16 [16, 2048, 768], P('expert', 'dp')
- down_grad: bfloat16 [16, 2048, 768], P('expert', 'dp')
- router_grad: float32 [2048, 16], replicated
Inputs may be any that keep to these rules, and one draw needn't show every extreme that they name: `expert_ids`: within the rows of one device (128 tokens, two experts each) no expert is named by more than 24 rows, and in some device some expert is named by exactly 24; a token names two different experts. placed is its own inverse, and placed[d] equals d or differs from d in exactly one bit.
All inputs are finite; a program needn't handle non-finite values.
Results may differ from a plain program's by a relative error of at most 0.018.
Values may be sent and summed in bfloat16 or wider, within the bound.
No kernel may reach another device: no remote copies, remote signals or barrier semaphores. Data moves between devices by JAX's collectives and lax.ppermute only.
A program may use at most 128 MiB of HBM per device.

v0:
```python
import jax
import jax.numpy as jnp
from jax import lax
from jax.sharding import PartitionSpec as P
from jax.experimental.layout import Layout, with_layout_constraint


def swapped(array, axis, stride):
    return lax.ppermute(array, axis, [(i, i ^ 1 << stride) for i in range(lax.axis_size(axis))])


def gather_by_exchange(piece, axis):
    count = lax.axis_size(axis)
    copies = jnp.broadcast_to(piece[None], (count,) + piece.shape)
    joined = lax.all_to_all(copies, axis, 0, 0, tiled=True)
    return joined.reshape((count * piece.shape[0],) + piece.shape[1:])


def reduce_router(term, companion, partner, my_index):
    groups = lax.axis_size("expert")
    replicas = lax.axis_size("dp")
    rows = term.shape[0]
    parts = lax.all_to_all(
        term.reshape(groups, rows // groups, term.shape[1]), "expert", 0, 0, tiled=True
    )
    piece = jnp.sum(parts, axis=0)
    piece, companion = lax.optimization_barrier((piece, companion))
    arrivals = [swapped(companion, "expert", bit_level) for bit_level in range(groups.bit_length() - 1)]
    for bit_level in range(replicas.bit_length() - 1):
        piece = piece + swapped(piece, "dp", bit_level)
    piece, arrivals = lax.optimization_barrier((piece, arrivals))
    chosen = companion
    for bit_level, arrived in enumerate(arrivals):
        chosen = jnp.where(partner == jnp.bitwise_xor(my_index, 1 << bit_level), arrived, chosen)
    return gather_by_exchange(piece, "expert"), chosen


def gate_values(logits, picked):
    scores = jax.nn.sigmoid(logits)
    chosen = jnp.sum(scores[:, None, :] * picked, axis=2)
    return chosen / jnp.sum(chosen, axis=1, keepdims=True)


def slot_numbers(expert_ids, holder, capacity, devices):
    labels = jnp.arange(devices, dtype=jnp.int32)
    member_e = (expert_ids[:, :, None] == labels[None, None, :]).astype(jnp.int32)
    target = jnp.sum(member_e * holder[None, None, :], axis=2)
    flat_target = target.reshape(-1)
    member = (flat_target[:, None] == labels[None, :]).astype(jnp.int32)
    ranking = jnp.sum((jnp.cumsum(member, axis=0) - 1) * member, axis=1)
    return (flat_target * capacity + ranking).reshape(expert_ids.shape)


def scatter_rows(per_pair, slot_index, total):
    flat_rows = per_pair.reshape(-1, per_pair.shape[2])
    empty = jnp.zeros((total, per_pair.shape[2]), per_pair.dtype)
    return empty.at[slot_index.reshape(-1)].set(flat_rows)


def expert_forward(slot_rows, gate_full, up_full, down_full):
    pre_gate = jnp.dot(slot_rows, gate_full, preferred_element_type=jnp.float32)
    pre_up = jnp.dot(slot_rows, up_full, preferred_element_type=jnp.float32)
    hidden = (jax.nn.silu(pre_gate) * pre_up).astype(jnp.bfloat16)
    result = lax.dot_general(
        hidden, down_full, (((1,), (1,)), ((), ())), preferred_element_type=jnp.float32
    )
    return (result.astype(jnp.bfloat16), pre_gate, pre_up, hidden)


def expert_backward(d_out, pre_gate, pre_up, gate_full, up_full, down_full):
    d_hidden = jnp.dot(d_out, down_full, preferred_element_type=jnp.float32)
    sigma = jax.nn.sigmoid(pre_gate)
    d_pre_gate = (d_hidden * pre_up * sigma * (1.0 + pre_gate * (1.0 - sigma))).astype(jnp.bfloat16)
    d_pre_up = (d_hidden * pre_gate * sigma).astype(jnp.bfloat16)
    back_dims = (((1,), (1,)), ((), ()))
    d_rows = lax.dot_general(d_pre_gate, gate_full, back_dims, preferred_element_type=jnp.float32)
    d_rows = d_rows + lax.dot_general(
        d_pre_up, up_full, back_dims, preferred_element_type=jnp.float32
    )
    return (d_rows.astype(jnp.bfloat16), d_pre_gate, d_pre_up)


def row_major(array):
    return with_layout_constraint(array, Layout(major_to_minor=tuple(range(array.ndim))))


def contract_rows(left, right):
    return lax.dot_general(
        left, right, (((0,), (0,)), ((), ())), preferred_element_type=jnp.float32
    )


def on_device(
    tokens, cotangent, expert_ids, placed, router_weight, gate_weight, up_weight, down_weight
):
    count = tokens.shape[0]
    width = tokens.shape[1]
    hid_width = gate_weight.shape[2]
    groups = lax.axis_size("expert")
    replicas = lax.axis_size("dp")
    capacity = 3 * count // groups
    total = groups * capacity
    levels = groups.bit_length() - 1
    my_index = lax.axis_index("expert")
    labels = jnp.arange(groups, dtype=jnp.int32)
    partner = jnp.sum(jnp.where(labels == my_index, placed, 0))
    grad_scale = (2.0 * count * replicas) ** (-0.5)
    router_scale = (1.0 * count * replicas * groups) ** (-0.5)
    logits = jnp.dot(tokens, router_weight, preferred_element_type=jnp.float32)
    picked = (expert_ids[:, :, None] == labels[None, None, :]).astype(jnp.float32)

    def gate_of(values):
        return gate_values(values, picked)

    gate_vals, gate_vjp = jax.vjp(gate_of, logits)
    held = jnp.concatenate([gate_weight, up_weight, down_weight], axis=0)
    gathered = lax.all_gather(held, "dp", axis=1, tiled=True)
    gate_full, up_full, down_full = (gathered[0], gathered[1], gathered[2])
    slot_index = slot_numbers(expert_ids, labels, capacity, groups)
    spread = jnp.broadcast_to(tokens[:, None, :], (count, 2, width))
    outbox = scatter_rows(spread, slot_index, total).reshape(groups, capacity, width)
    received = lax.all_to_all(outbox, "expert", split_axis=0, concat_axis=0, tiled=True)
    item_count = received.shape[1]
    forward_slot_rows = received.reshape(-1, width)
    result, pre_gate, pre_up, hidden = expert_forward(
        forward_slot_rows, gate_full, up_full, down_full
    )
    result, pre_gate, pre_up, hidden, inbox = (
        result.reshape(groups, item_count, width),
        pre_gate.reshape(groups, item_count, hid_width),
        pre_up.reshape(groups, item_count, hid_width),
        hidden.reshape(groups, item_count, hid_width),
        received,
    )
    returned = lax.all_to_all(result, "expert", split_axis=0, concat_axis=0, tiled=True).reshape(
        total, width
    )
    expert_out = returned[slot_index].astype(jnp.float32)
    mixed = jnp.sum(gate_vals[:, :, None] * expert_out, axis=1).astype(jnp.bfloat16)
    cot_wide = cotangent.astype(jnp.float32)
    d_gates = jnp.sum(cot_wide[:, None, :] * expert_out, axis=2)
    d_out = (gate_vals[:, :, None] * cot_wide[:, None, :]).astype(jnp.bfloat16)
    d_outbox = scatter_rows(d_out, slot_index, total).reshape(groups, capacity, width)
    d_inbox = lax.all_to_all(d_outbox, "expert", split_axis=0, concat_axis=0, tiled=True).reshape(
        total, width
    )
    gate_back, up_back, down_back = (gate_full, up_full, down_full)
    slot_rows = inbox.reshape(total, width)
    hidden_rows = hidden.reshape(total, hid_width)
    d_rows, d_pre_gate, d_pre_up = expert_backward(
        d_inbox,
        pre_gate.reshape(total, hid_width),
        pre_up.reshape(total, hid_width),
        gate_back,
        up_back,
        down_back,
    )
    d_returned = lax.all_to_all(
        d_rows.reshape(groups, capacity, width), "expert", split_axis=0, concat_axis=0, tiled=True
    ).reshape(total, width)
    d_expert = jnp.sum(d_returned[slot_index].astype(jnp.float32), axis=1)
    pieces = [
        row_major(contract_rows(slot_rows, d_pre_gate)),
        row_major(contract_rows(slot_rows, d_pre_up)),
        row_major(contract_rows(d_inbox, hidden_rows)),
    ]
    shares = lax.psum_scatter(
        (jnp.concatenate(pieces, axis=1) * grad_scale).astype(jnp.bfloat16),
        "dp",
        scatter_dimension=0,
        tiled=True,
    ).astype(jnp.float32)
    grad_stack = jnp.stack(
        [shares[:, :hid_width], shares[:, hid_width : 2 * hid_width], shares[:, 2 * hid_width :]],
        axis=0,
    ).astype(jnp.bfloat16)
    d_logits = gate_vjp(d_gates)[0].astype(jnp.bfloat16)
    router_term = contract_rows(tokens, d_logits) * router_scale
    router_grad, grad_stack = reduce_router(router_term, grad_stack, partner, my_index)
    router_back = lax.dot_general(
        d_logits, router_weight, (((1,), (1,)), ((), ())), preferred_element_type=jnp.float32
    )
    token_grad = (d_expert + router_back).astype(jnp.bfloat16)
    return (mixed, token_grad, grad_stack[0:1], grad_stack[1:2], grad_stack[2:3], router_grad)


def solution(mesh):
    in_specs = (
        P(("dp", "expert"), None),
        P(("dp", "expert"), None),
        P(("dp", "expert"), None),
        P(),
        P(),
        P("expert", "dp", None),
        P("expert", "dp", None),
        P("expert", "dp", None),
    )
    out_specs = (
        P(("dp", "expert"), None),
        P(("dp", "expert"), None),
        P("expert", "dp", None),
        P("expert", "dp", None),
        P("expert", "dp", None),
        P(),
    )
    return jax.shard_map(
        on_device, mesh=mesh, in_specs=in_specs, out_specs=out_specs, check_vma=False
    )
```

profile of v0, /device:TPU:2, one launch (start us, length us, event | category | flops | bytes accessed | tf_op | source)
XLA Modules:
  0.0 226.4 jit_solution(10114832078988708128)
XLA Ops:
  13.5 4.1 %scatter_custom_fusion = bf16[384,2048]{1,0:T(8,128)(2,1)} fusion(s32[256]{0:T(256)S(1)} %bitcast.92, bf16[256,2048]{1,0:T(8,128)(2,1)} %reshape.199, bf16[]{:T(256)} %constant.16.clone.1), kind=kCustom, calls=%fused_computation.33 | custom fusion | bytes 1573376 | tf_op jit(solution)/shard_map/scatter | solution.py:57
  17.6 7.5 %all-to-all-start = ((bf16[16,24,2048]{2,1,0:T(8,128)(2,1)}), bf16[16,24,2048]{2,1,0:T(8,128)(2,1)S(1)}, u32[]{:S(2)}, u32[]{:S(2)}) async-start(bf16[16,24,2048]{2,1,0:T(8,128)(2,1)} %bitcast.3), calls=%async_computation | async-start | bytes 3145728 | tf_op jit(solution)/shard_map/all_to_all | solution.py:122
  25.1 2.5 %mul.155 = f32[128,2,2048]{2,1,0:T(2,128)} broadcast(bf16[128,2048]{1,0:T(8,128)(2,1)S(1)} %copy-done.3), dimensions={0,2} | broadcast | bytes 2621440 | tf_op jit(solution)/shard_map/mul | solution.py:142
  27.6 3.7 %mul.156 = f32[256,2048]{1,0:T(8,128)} reshape(f32[128,2,2048]{2,1,0:T(2,128)} %mul.155) | data formatting | bytes 4194304 | tf_op jit(solution)/shard_map/mul | solution.py:142
  31.8 4.6 %scatter_custom_fusion.1 = bf16[384,2048]{1,0:T(8,128)(2,1)} fusion(s32[256]{0:T(256)S(1)} %bitcast.93, f32[256,2048]{1,0:T(8,128)} %mul.156, f32[256]{0:T(256)S(1)} %div.42, bf16[]{:T(256)} %constant.16.clone.1), kind=kCustom, calls=%fused_computation.30 | custom fusion | flops 1048576 | bytes 3671042 | tf_op jit(solution)/shard_map/scatter | solution.py:57
  36.4 10.1 %all-to-all-done = bf16[16,24,2048]{2,1,0:T(8,128)(2,1)S(1)} async-done(((bf16[16,24,2048]{2,1,0:T(8,128)(2,1)}), bf16[16,24,2048]{2,1,0:T(8,128)(2,1)S(1)}, u32[]{:S(2)}, u32[]{:S(2)}) %all-to-all-start) | async-done | bytes 1572896 | tf_op jit(solution)/shard_map/all_to_all | solution.py:122
  46.5 6.3 %all-to-all-start.2 = ((bf16[16,24,2048]{2,1,0:T(8,128)(2,1)}), bf16[16,24,2048]{2,1,0:T(8,128)(2,1)S(1)}, u32[]{:S(2)}, u32[]{:S(2)}) async-start(bf16[16,24,2048]{2,1,0:T(8,128)(2,1)} %bitcast.88), calls=%async_computation.2 | async-start | bytes 3145728 | tf_op jit(solution)/shard_map/all_to_all | solution.py:144
  53.0 20.6 %all-gather.2.cloned.1.call-done = bf16[3,2048,768]{2,1,0:T(8,128)(2,1)} async-done(((bf16[3,128,768]{2,1,0:T(8,128)(2,1)}), bf16[3,2048,768]{2,1,0:T(8,128)(2,1)}) %all-gather.2.cloned.1.call-update) | async-done | bytes 9437200 | tf_op jit(solution)/shard_map/all_gather | solution.py:117
  73.6 4.3 %fusion.2 = f32[384,768]{1,0:T(8,128)} fusion(bf16[384,2048]{1,0:T(8,128)(2,1)S(1)} %bitcast.82, bf16[3,2048,768]{2,1,0:T(8,128)(2,1)} %all-gather.2.cloned.1.call-done), kind=kOutput, calls=%fused_computation.12 | convolution fusion | flops 1207959552 | bytes 5898240 | tf_op jit(solution)/shard_map/dot_general | solution.py:61
  77.9 4.3 %fusion.3 = f32[384,768]{1,0:T(8,128)} fusion(bf16[384,2048]{1,0:T(8,128)(2,1)S(1)} %bitcast.83, bf16[3,2048,768]{2,1,0:T(8,128)(2,1)} %all-gather.2.cloned.1.call-done), kind=kOutput, calls=%fused_computation.13 | convolution fusion | flops 1207959552 | bytes 5898240 | tf_op jit(solution)/shard_map/dot_general | solution.py:62
  82.2 4.2 %multiply_convert_fusion.1 = (bf16[384,768]{1,0:T(8,128)(2,1)S(1)}, bf16[384,768]{1,0:T(8,128)(2,1)S(1)}, bf16[384,768]{1,0:T(8,128)(2,1)S(1)}) fusion(f32[384,768]{1,0:T(8,128)} %fusion.2, f32[384,768]{1,0:T(8,128)} %fusion.3, bf16[384,2048]{1,0:T(8,128)(2,1)S(1)} %bitcast.86, bf16[3,2048,768]{2,1,0:T(8,128)(2,1)} %all-gather.2.cloned.1.call-done), kind=kOutput, calls=%fused_computation.21 | convolution fusion | flops 1212678144 | bytes 8847360 | tf_op jit(solution)/shard_map/dot_general | solution.py:71
  92.0 4.6 %fusion = bf16[2048,2304]{1,0:T(8,128)(2,1)} fusion(f32[2048,768]{1,0:T(8,128)S(1)} %fusion.24, f32[2048,768]{1,0:T(8,128)S(1)} %fusion.23, f32[2048,768]{1,0:T(8,128)S(1)} %fusion.22), kind=kLoop, calls=%fused_computation.5 | loop fusion | flops 18874368 | bytes 28311552 | tf_op jit(solution)/shard_map/convert_element_type | solution.py:168
  97.8 4.5 %convolution_convert_fusion = bf16[384,2048]{1,0:T(8,128)(2,1)} fusion(bf16[384,768]{1,0:T(8,128)(2,1)S(1)} %copy-done.10, bf16[3,2048,768]{2,1,0:T(8,128)(2,1)} %all-gather.2.cloned.1.call-done), kind=kOutput, calls=%fused_computation.10 | convolution fusion | flops 1208745984 | bytes 5308416 | tf_op jit(solution)/shard_map/dot_general | solution.py:64
  102.3 7.4 %all-to-all-start.1 = ((bf16[16,24,2048]{2,1,0:T(8,128)(2,1)}), bf16[16,24,2048]{2,1,0:T(8,128)(2,1)S(1)}, u32[]{:S(2)}, u32[]{:S(2)}) async-start(bf16[16,24,2048]{2,1,0:T(8,128)(2,1)} %bitcast.90), calls=%async_computation.1 | async-start | bytes 3145728 | tf_op jit(solution)/shard_map/all_to_all | solution.py:135
  111.3 5.1 %fusion.1 = f32[384,2048]{1,0:T(8,128)} fusion(bf16[384,768]{1,0:T(8,128)(2,1)S(1)} %copy-done.8, bf16[3,2048,768]{2,1,0:T(8,128)(2,1)} %all-gather.2.cloned.1.call-done), kind=kOutput, calls=%fused_computation.11 | convolution fusion | flops 1207959552 | bytes 6881280 | tf_op jit(solution)/shard_map/dot_general | solution.py:76
  116.3 15.2 %all-to-all-done.1 = bf16[16,24,2048]{2,1,0:T(8,128)(2,1)S(1)} async-done(((bf16[16,24,2048]{2,1,0:T(8,128)(2,1)}), bf16[16,24,2048]{2,1,0:T(8,128)(2,1)S(1)}, u32[]{:S(2)}, u32[]{:S(2)}) %all-to-all-start.1) | async-done | bytes 1572896 | tf_op jit(solution)/shard_map/all_to_all | solution.py:135
  131.5 2.4 %gather_fusion = bf16[256,2048]{1,0:T(8,128)(2,1)} fusion(bf16[384,2048]{1,0:T(8,128)(2,1)S(1)} %bitcast.81, s32[1024]{0:T(1024)S(1)} %pad_clamp_fusion), kind=kCustom, calls=%fused_computation | custom fusion | bytes 2098176 | tf_op jit(solution)/shard_map/gather | solution.py:138
  133.9 2.4 %reshape.213 = f32[128,2,2048]{2,1,0:T(2,128)S(1)} reshape(bf16[256,2048]{1,0:T(8,128)(2,1)} %gather_fusion) | data formatting | bytes 3145728 | tf_op jit(solution)/shard_map/convert_element_type | solution.py:138
  136.3 6.0 %multiply_reduce_fusion = (f32[128,2]{1,0:T(8,128)S(1)}, bf16[128,2048]{1,0:T(8,128)(2,1)}) fusion(f32[128,2,2048]{2,1,0:T(2,128)S(1)} %reshape.213, f32[128,2048]{1,0:T(8,128)} %convert_element_type.54, f32[128,2]{1,0:T(8,128)S(1)} %copy.38), kind=kLoop, calls=%fused_computation.18 | loop fusion | flops 1834752 | bytes 3672064 | tf_op jit(solution)/shard_map/reduce_sum | solution.py:141
  143.4 6.3 %all-to-all-start.4 = ((f32[16,128,16]{1,2,0:T(8,128)}), f32[16,128,16]{1,2,0:T(8,128)S(1)}, u32[]{:S(2)}, u32[]{:S(2)}) async-start(f32[16,128,16]{1,2,0:T(8,128)} %bitcast.79), calls=%async_computation.4 | async-start | bytes 262144 | tf_op jit(solution)/shard_map/all_to_all | solution.py:23
  149.7 5.6 %add_convert_fusion = bf16[384,2048]{1,0:T(8,128)(2,1)} fusion(f32[384,2048]{1,0:T(8,128)} %fusion.1, bf16[384,768]{1,0:T(8,128)(2,1)S(1)} %copy-done.6, bf16[3,2048,768]{2,1,0:T(8,128)(2,1)} %all-gather.2.cloned.1.call-done), kind=kOutput, calls=%fused_computation.9 | convolution fusion | flops 1209532416 | bytes 8454144 | tf_op jit(solution)/shard_map/dot_general | solution.py:77
  156.1 6.6 %all-to-all-start.3 = ((bf16[16,24,2048]{2,1,0:T(8,128)(2,1)}), bf16[16,24,2048]{2,1,0:T(8,128)(2,1)S(1)}, u32[]{:S(2)}, u32[]{:S(2)}) async-start(bf16[16,24,2048]{2,1,0:T(8,128)(2,1)} %bitcast.89), calls=%async_computation.3 | async-start | bytes 3145728 | tf_op jit(solution)/shard_map/all_to_all | solution.py:158
  162.7 6.0 %reduce-scatter.2.cloned.1.call-done = bf16[128,2304]{1,0:T(8,128)(2,1)} async-done(((bf16[2048,2304]{1,0:T(8,128)(2,1)}), bf16[128,2304]{1,0:T(8,128)(2,1)}) %reduce-scatter.2.cloned.1.call-update) | async-done | bytes 589840 | tf_op jit(solution)/shard_map/reduce_scatter | solution.py:167
  172.2 2.7 %collective-permute-start.5 = (bf16[3,128,768]{2,1,0:T(8,128)(2,1)}, bf16[3,128,768]{2,1,0:T(8,128)(2,1)}, u32[]{:S(2)}, u32[]{:S(2)}) collective-permute-start(bf16[3,128,768]{2,1,0:T(8,128)(2,1)} %pad_maximum_fusion.1), channel_id=1, source_target_pairs={{0,2},{1,3},{2,0},{3,1},{4,6},{5,7},{6,4},{7,5},{8,10},{9,11},{10,... | collective-permute-start | bytes 1769480 | tf_op jit(solution)/shard_map/ppermute | solution.py:9
  178.9 3.6 %collective-permute-done.1 = f32[128,16]{0,1:T(8,128)S(1)} collective-permute-done((f32[128,16]{0,1:T(8,128)S(1)}, f32[128,16]{0,1:T(8,128)S(1)}, u32[]{:S(2)}, u32[]{:S(2)}) %collective-permute-start.1) | collective-permute-done | bytes 8224 | tf_op jit(solution)/shard_map/ppermute | solution.py:9
  189.2 2.4 %reshape.214 = f32[128,2,2048]{2,1,0:T(2,128)S(1)} reshape(bf16[256,2048]{1,0:T(8,128)(2,1)} %gather_fusion.1) | data formatting | bytes 3145728 | tf_op jit(solution)/shard_map/convert_element_type | solution.py:161
  191.6 2.8 %reduce_sum.118 = f32[128,2048]{1,0:T(8,128)S(1)} reduce(f32[128,2,2048]{2,1,0:T(2,128)S(1)} %reshape.214, f32[]{:T(128)} %constant.15.clone.1), dimensions={1}, to_apply=%region_9.10 | reduce | flops 262144 | bytes 3145732 | tf_op jit(solution)/shard_map/reduce_sum | solution.py:161
  194.3 2.9 %collective-permute-start.3 = (f32[128,16]{0,1:T(8,128)S(1)}, f32[128,16]{0,1:T(8,128)S(1)}, u32[]{:S(2)}, u32[]{:S(2)}) collective-permute-start(f32[128,16]{0,1:T(8,128)S(1)} %add.87), channel_id=1, source_target_pairs={{0,128},{16,144},{32,160},{48,176},{64,192},{80,208},{96,224},{112... | collective-permute-start | bytes 24584 | tf_op jit(solution)/shard_map/ppermute | solution.py:9
  198.4 3.6 %collective-permute-done.3 = f32[128,16]{0,1:T(8,128)S(1)} collective-permute-done((f32[128,16]{0,1:T(8,128)S(1)}, f32[128,16]{0,1:T(8,128)S(1)}, u32[]{:S(2)}, u32[]{:S(2)}) %collective-permute-start.3) | collective-permute-done | bytes 8224 | tf_op jit(solution)/shard_map/ppermute | solution.py:9
  202.0 4.4 %collective-permute-done.5 = bf16[3,128,768]{2,1,0:T(8,128)(2,1)} collective-permute-done((bf16[3,128,768]{2,1,0:T(8,128)(2,1)}, bf16[3,128,768]{2,1,0:T(8,128)(2,1)}, u32[]{:S(2)}, u32[]{:S(2)}) %collective-permute-start.5) | collective-permute-done | bytes 589856 | tf_op jit(solution)/shard_map/ppermute | solution.py:9
  207.7 4.8 %all-to-all-start.5 = ((f32[16,128,16]{1,2,0:T(8,128)}), f32[16,128,16]{1,2,0:T(8,128)S(1)}, u32[]{:S(2)}, u32[]{:S(2)}) async-start(f32[16,128,16]{1,2,0:T(8,128)} %broadcast_in_dim.19), calls=%async_computation.6 | async-start | bytes 262144 | tf_op jit(solution)/shard_map/all_to_all | solution.py:15
  214.5 4.4 %all-to-all-done.5 = f32[16,128,16]{1,2,0:T(8,128)S(1)} async-done(((f32[16,128,16]{1,2,0:T(8,128)}), f32[16,128,16]{1,2,0:T(8,128)S(1)}, u32[]{:S(2)}, u32[]{:S(2)}) %all-to-all-start.5) | async-done | bytes 131104 | tf_op jit(solution)/shard_map/all_to_all | solution.py:15
  (99 shorter events, 33.6 us)
Async XLA Ops:
  7.2 24.1 %copy-start = (bf16[2048,16]{0,1:T(8,128)(2,1)S(1)}, bf16[2048,16]{0,1:T(8,128)(2,1)}, u32[]{:S(2)}) copy-start(bf16[2048,16]{0,1:T(8,128)(2,1)} %param.12) | copy-start | bytes 196612
  7.2 4.4 %copy-start.1 = (bf16[128,2048]{1,0:T(8,128)(2,1)S(1)}, bf16[128,2048]{1,0:T(8,128)(2,1)}, u32[]{:S(2)}) copy-start(bf16[128,2048]{1,0:T(8,128)(2,1)} %param.8) | copy-start | bytes 1572868
  7.2 66.4 %all-gather.2.cloned.1.call-start = ((), (), s32[]{:S(2)}) async-start(), calls=%async_computation.7 | async-start | bytes 10027008 | tf_op jit(solution)/shard_map/all_gather | solution.py:117
  13.5 11.6 %copy-start.3 = (bf16[128,2048]{1,0:T(8,128)(2,1)S(1)}, bf16[128,2048]{1,0:T(8,128)(2,1)}, u32[]{:S(2)}) copy-start(bf16[128,2048]{1,0:T(8,128)(2,1)} %param.9) | copy-start | bytes 1572868
  17.6 28.9 %all-to-all-start = ((bf16[16,24,2048]{2,1,0:T(8,128)(2,1)}), bf16[16,24,2048]{2,1,0:T(8,128)(2,1)S(1)}, u32[]{:S(2)}, u32[]{:S(2)}) async-start(bf16[16,24,2048]{2,1,0:T(8,128)(2,1)} %bitcast.3), calls=%async_computation | async-start | bytes 3145728 | tf_op jit(solution)/shard_map/all_to_all | solution.py:122
  27.6 3.9 %copy-start.11 = (s32[128,2]{0,1:T(2,128)S(1)}, s32[128,2]{0,1:T(2,128)}, u32[]{:S(2)}) copy-start(s32[128,2]{0,1:T(2,128)} %param.10) | copy-start | bytes 3076
  46.5 35.7 %all-to-all-start.2 = ((bf16[16,24,2048]{2,1,0:T(8,128)(2,1)}), bf16[16,24,2048]{2,1,0:T(8,128)(2,1)S(1)}, u32[]{:S(2)}, u32[]{:S(2)}) async-start(bf16[16,24,2048]{2,1,0:T(8,128)(2,1)} %bitcast.88), calls=%async_computation.2 | async-start | bytes 3145728 | tf_op jit(solution)/shard_map/all_to_all | solution.py:144
  52.8 116.0 %reduce-scatter.2.cloned.1.call-start = ((), (), s32[]{:S(2)}) async-start(), calls=%async_computation.8 | async-start | bytes 10027008 | tf_op jit(solution)/shard_map/reduce_scatter | solution.py:167
  86.4 1.9 copy-start.9
  86.4 1.9 copy-start.5
  86.4 3.7 %copy-start.7 = (bf16[384,768]{1,0:T(8,128)(2,1)}, bf16[384,768]{1,0:T(8,128)(2,1)S(1)}, u32[]{:S(2)}) copy-start(bf16[384,768]{1,0:T(8,128)(2,1)S(1)} %get-tuple-element.25) | copy-start | bytes 1769476
  96.7 1.1 copy-start.10
  102.3 7.6 %copy-start.4 = (bf16[128,2048]{1,0:T(8,128)(2,1)S(1)}, bf16[128,2048]{1,0:T(8,128)(2,1)}, u32[]{:S(2)}) copy-start(bf16[128,2048]{1,0:T(8,128)(2,1)} %param.9) | copy-start | bytes 1572868
  102.3 9.0 %copy-start.8 = (bf16[384,768]{1,0:T(8,128)(2,1)S(1)}, bf16[384,768]{1,0:T(8,128)(2,1)}, u32[]{:S(2)}) copy-start(bf16[384,768]{1,0:T(8,128)(2,1)} %copy-done.7) | copy-start | bytes 1769476
  102.3 29.2 %all-to-all-start.1 = ((bf16[16,24,2048]{2,1,0:T(8,128)(2,1)}), bf16[16,24,2048]{2,1,0:T(8,128)(2,1)S(1)}, u32[]{:S(2)}, u32[]{:S(2)}) async-start(bf16[16,24,2048]{2,1,0:T(8,128)(2,1)} %bitcast.90), calls=%async_computation.1 | async-start | bytes 3145728 | tf_op jit(solution)/shard_map/all_to_all | solution.py:135
  136.3 6.2 %copy-start.2 = (bf16[128,2048]{1,0:T(8,128)(2,1)S(1)}, bf16[128,2048]{1,0:T(8,128)(2,1)}, u32[]{:S(2)}) copy-start(bf16[128,2048]{1,0:T(8,128)(2,1)} %param.8) | copy-start | bytes 1572868
  136.3 13.4 %copy-start.6 = (bf16[384,768]{1,0:T(8,128)(2,1)S(1)}, bf16[384,768]{1,0:T(8,128)(2,1)}, u32[]{:S(2)}) copy-start(bf16[384,768]{1,0:T(8,128)(2,1)} %copy-done.5) | copy-start | bytes 1769476
  143.4 12.7 %all-to-all-start.4 = ((f32[16,128,16]{1,2,0:T(8,128)}), f32[16,128,16]{1,2,0:T(8,128)S(1)}, u32[]{:S(2)}, u32[]{:S(2)}) async-start(f32[16,128,16]{1,2,0:T(8,128)} %bitcast.79), calls=%async_computation.4 | async-start | bytes 262144 | tf_op jit(solution)/shard_map/all_to_all | solution.py:23
  156.1 27.5 %copy-start.12 = (s32[16]{0:T(128)S(1)}, s32[16]{0:T(128)}, u32[]{:S(2)}) copy-start(s32[16]{0:T(128)} %param.11) | copy-start | bytes 196
  156.1 30.7 %all-to-all-start.3 = ((bf16[16,24,2048]{2,1,0:T(8,128)(2,1)}), bf16[16,24,2048]{2,1,0:T(8,128)(2,1)S(1)}, u32[]{:S(2)}, u32[]{:S(2)}) async-start(bf16[16,24,2048]{2,1,0:T(8,128)(2,1)} %bitcast.89), calls=%async_computation.3 | async-start | bytes 3145728 | tf_op jit(solution)/shard_map/all_to_all | solution.py:158
  170.8 31.2 %collective-permute-start.4 = (bf16[3,128,768]{2,1,0:T(8,128)(2,1)}, bf16[3,128,768]{2,1,0:T(8,128)(2,1)}, u32[]{:S(2)}, u32[]{:S(2)}) collective-permute-start(bf16[3,128,768]{2,1,0:T(8,128)(2,1)} %pad_maximum_fusion.1), channel_id=1, source_target_pairs={{0,1},{1,0},{2,3},{3,2},{4,5},{5,4},{6,7},{7,6},{8,9},{9,8},{10,11... | collective-permute-start | bytes 1769480 | tf_op jit(solution)/shard_map/ppermute | solution.py:9
  172.2 34.1 %collective-permute-start.5 = (bf16[3,128,768]{2,1,0:T(8,128)(2,1)}, bf16[3,128,768]{2,1,0:T(8,128)(2,1)}, u32[]{:S(2)}, u32[]{:S(2)}) collective-permute-start(bf16[3,128,768]{2,1,0:T(8,128)(2,1)} %pad_maximum_fusion.1), channel_id=1, source_target_pairs={{0,2},{1,3},{2,0},{3,1},{4,6},{5,7},{6,4},{7,5},{8,10},{9,11},{10,... | collective-permute-start | bytes 1769480 | tf_op jit(solution)/shard_map/ppermute | solution.py:9
  175.0 31.4 %collective-permute-start.6 = (bf16[3,128,768]{2,1,0:T(8,128)(2,1)}, bf16[3,128,768]{2,1,0:T(8,128)(2,1)}, u32[]{:S(2)}, u32[]{:S(2)}) collective-permute-start(bf16[3,128,768]{2,1,0:T(8,128)(2,1)} %pad_maximum_fusion.1), channel_id=1, source_target_pairs={{0,4},{1,5},{2,6},{3,7},{4,0},{5,1},{6,2},{7,3},{8,12},{9,13},{10,... | collective-permute-start | bytes 1769480 | tf_op jit(solution)/shard_map/ppermute | solution.py:9
  175.5 31.5 %collective-permute-start.7 = (bf16[3,128,768]{2,1,0:T(8,128)(2,1)}, bf16[3,128,768]{2,1,0:T(8,128)(2,1)}, u32[]{:S(2)}, u32[]{:S(2)}) collective-permute-start(bf16[3,128,768]{2,1,0:T(8,128)(2,1)} %pad_maximum_fusion.1), channel_id=1, source_target_pairs={{0,8},{1,9},{2,10},{3,11},{4,12},{5,13},{6,14},{7,15},{8,0},{9,1},... | collective-permute-start | bytes 1769480 | tf_op jit(solution)/shard_map/ppermute | solution.py:9
  177.8 1.2 collective-permute-start
  178.9 3.7 %collective-permute-start.1 = (f32[128,16]{0,1:T(8,128)S(1)}, f32[128,16]{0,1:T(8,128)S(1)}, u32[]{:S(2)}, u32[]{:S(2)}) collective-permute-start(f32[128,16]{0,1:T(8,128)S(1)} %add.85), channel_id=1, source_target_pairs={{0,32},{16,48},{32,0},{48,16},{64,96},{80,112},{96,64},{112,80},{1... | collective-permute-start | bytes 24584 | tf_op jit(solution)/shard_map/ppermute | solution.py:9
  182.6 11.7 %collective-permute-start.2 = (f32[128,16]{0,1:T(8,128)S(1)}, f32[128,16]{0,1:T(8,128)S(1)}, u32[]{:S(2)}, u32[]{:S(2)}) collective-permute-start(f32[128,16]{0,1:T(8,128)S(1)} %add.86), channel_id=1, source_target_pairs={{0,64},{16,80},{32,96},{48,112},{64,0},{80,16},{96,32},{112,48},{1... | collective-permute-start | bytes 24584 | tf_op jit(solution)/shard_map/ppermute | solution.py:9
  194.3 7.6 %collective-permute-start.3 = (f32[128,16]{0,1:T(8,128)S(1)}, f32[128,16]{0,1:T(8,128)S(1)}, u32[]{:S(2)}, u32[]{:S(2)}) collective-permute-start(f32[128,16]{0,1:T(8,128)S(1)} %add.87), channel_id=1, source_target_pairs={{0,128},{16,144},{32,160},{48,176},{64,192},{80,208},{96,224},{112... | collective-permute-start | bytes 24584 | tf_op jit(solution)/shard_map/ppermute | solution.py:9
  207.7 11.2 %all-to-all-start.5 = ((f32[16,128,16]{1,2,0:T(8,128)}), f32[16,128,16]{1,2,0:T(8,128)S(1)}, u32[]{:S(2)}, u32[]{:S(2)}) async-start(f32[16,128,16]{1,2,0:T(8,128)} %broadcast_in_dim.19), calls=%async_computation.6 | async-start | bytes 262144 | tf_op jit(solution)/shard_map/all_to_all | solution.py:15
Sparse Core Ops, SparseCore 0:
  9.9 63.7 all-gather.1
  96.8 71.8 reduce-scatter.1
where the time goes:
time: 227 us; the launch traced here: 226 us
  waiting for transfers between devices  70.5 us (31%)
  starting transfers between devices  50.1 us (22%)
  matrix products  35 us (15%)
  local copies, waits for them, and re-layouts  28.2 us (12%)
  other arithmetic  25.5 us (11%)
  between operations  17 us (7%)
    all_gather x1, waiting for transfers between devices, on_device(): gathered = lax.all_gather(held, 'dp', axis=1, tiled=True)  20.6 us
    all_to_all x1, waiting for transfers between devices, on_device(): lax.all_to_all(result, 'expert', split_axis=0, concat_axis=0, tiled=True)  15.2 us
    ppermute x8, waiting for transfers between devices, swapped(): lax.ppermute(array, axis, [(i, i ^ 1 << stride) for i in range(lax.axis_s...  13.5 us
    ppermute x8, starting transfers between devices, swapped(): lax.ppermute(array, axis, [(i, i ^ 1 << stride) for i in range(lax.axis_s...  10.9 us
    all_to_all x1, waiting for transfers between devices, on_device(): lax.all_to_all(outbox, 'expert', split_axis=0, concat_axis=0, tiled=True)  10.1 us
    all_to_all x1, starting transfers between devices, on_device(): lax.all_to_all(outbox, 'expert', split_axis=0, concat_axis=0, tiled=True)  7.48 us
    all_to_all x1, starting transfers between devices, on_device(): lax.all_to_all(result, 'expert', split_axis=0, concat_axis=0, tiled=True)  7.41 us
    all_to_all x1, starting transfers between devices, on_device(): lax.all_to_all(d_rows.reshape(groups, capacity, width), 'expert', split_a...  6.59 us
  transfers between devices with their start and end apart: 16, of which 11 were waited for; matrix products, arithmetic and copies ran while one was open for 31% of the time, Pallas kernels for 0%

commit v1 on v0

--- a/solution.py
+++ b/solution.py
@@ -24,15 +24,16 @@
         term.reshape(groups, rows // groups, term.shape[1]), "expert", 0, 0, tiled=True
     )
     piece = jnp.sum(parts, axis=0)
+    for bit_level in range(replicas.bit_length() - 1):
+        piece = piece + swapped(piece, "dp", bit_level)
     piece, companion = lax.optimization_barrier((piece, companion))
     arrivals = [swapped(companion, "expert", bit_level) for bit_level in range(groups.bit_length() - 1)]
-    for bit_level in range(replicas.bit_length() - 1):
-        piece = piece + swapped(piece, "dp", bit_level)
-    piece, arrivals = lax.optimization_barrier((piece, arrivals))
+    whole = gather_by_exchange(piece, "expert")
+    whole, arrivals = lax.optimization_barrier((whole, arrivals))
     chosen = companion
     for bit_level, arrived in enumerate(arrivals):
         chosen = jnp.where(partner == jnp.bitwise_xor(my_index, 1 << bit_level), arrived, chosen)
-    return gather_by_exchange(piece, "expert"), chosen
+    return whole, chosen
 
 
 def gate_values(logits, picked):

time: 227 us -> 231 us (1.018)
  waiting for transfers between devices: 70.5 us -> 74.7 us
    all_to_all x1, waiting for transfers between devices: 4.36 us -> 16.1 us  [gather_by_exchange(): joined = lax.all_to_all(copies, axis, 0, 0, tiled=True)]
    reduce_scatter x1, waiting for transfers between devices: 6.05 us -> 0.02 us  [on_device(): lax.psum_scatter((jnp.concatenate(pieces, axis=1) * grad_scale).astype(jn...]
    ppermute x8, waiting for transfers between devices: 13.5 us -> 8.02 us  [swapped(): lax.ppermute(array, axis, [(i, i ^ 1 << stride) for i in range(lax.axis_s...]
    all_to_all x1, waiting for transfers between devices: 0.01 us -> 3.86 us  [on_device(): lax.all_to_all(d_rows.reshape(groups, capacity, width), 'expert', split_a...]
  transfers between devices with their start and end apart: 16 -> 16, of which waited for: 11 -> 9; matrix products, arithmetic and copies ran while one was open for 31% -> 29% of each run, Pallas kernels for 0% -> 0%
where the time goes in v1:
time: 231 us; the launch traced here: 230 us
  waiting for transfers between devices  74.7 us (32%)
  starting transfers between devices  51 us (22%)
  matrix products  35 us (15%)
  local copies, waits for them, and re-layouts  28.2 us (12%)
  other arithmetic  23.6 us (10%)
  between operations  17 us (7%)
    all_gather x1, waiting for transfers between devices, on_device(): gathered = lax.all_gather(held, 'dp', axis=1, tiled=True)  20.6 us
    all_to_all x1, waiting for transfers between devices, gather_by_exchange(): joined = lax.all_to_all(copies, axis, 0, 0, tiled=True)  16.1 us
    all_to_all x1, waiting for transfers between devices, on_device(): lax.all_to_all(result, 'expert', split_axis=0, concat_axis=0, tiled=True)  15.2 us
    ppermute x8, starting transfers between devices, swapped(): lax.ppermute(array, axis, [(i, i ^ 1 << stride) for i in range(lax.axis_s...  10.1 us
    all_to_all x1, waiting for transfers between devices, on_device(): lax.all_to_all(outbox, 'expert', split_axis=0, concat_axis=0, tiled=True)  10.1 us
    ppermute x8, waiting for transfers between devices, swapped(): lax.ppermute(array, axis, [(i, i ^ 1 << stride) for i in range(lax.axis_s...  8.02 us
    all_to_all x1, starting transfers between devices, on_device(): lax.all_to_all(outbox, 'expert', split_axis=0, concat_axis=0, tiled=True)  7.48 us
    all_to_all x1, starting transfers between devices, on_device(): lax.all_to_all(result, 'expert', split_axis=0, concat_axis=0, tiled=True)  7.41 us
  transfers between devices with their start and end apart: 16, of which 9 were waited for; matrix products, arithmetic and copies ran while one was open for 29% of the time, Pallas kernels for 0%

profile of v1, /device:TPU:2, one launch (start us, length us, event | category | flops | bytes accessed | tf_op | source)
XLA Modules:
  0.0 229.6 jit_solution(5287425861332917408)
XLA Ops:
  7.2 2.1 pad_maximum_fusion
  13.5 4.1 %scatter_custom_fusion = bf16[384,2048]{1,0:T(8,128)(2,1)} fusion(s32[256]{0:T(256)S(1)} %bitcast.92, bf16[256,2048]{1,0:T(8,128)(2,1)} %reshape.199, bf16[]{:T(256)} %constant.16.clone.1), kind=kCustom, calls=%fused_computation.33 | custom fusion | bytes 1573376 | tf_op jit(solution)/shard_map/scatter | solution.py:58
  17.6 7.5 %all-to-all-start = ((bf16[16,24,2048]{2,1,0:T(8,128)(2,1)}), bf16[16,24,2048]{2,1,0:T(8,128)(2,1)S(1)}, u32[]{:S(2)}, u32[]{:S(2)}) async-start(bf16[16,24,2048]{2,1,0:T(8,128)(2,1)} %bitcast.3), calls=%async_computation | async-start | bytes 3145728 | tf_op jit(solution)/shard_map/all_to_all | solution.py:123
  25.1 2.5 %mul.155 = f32[128,2,2048]{2,1,0:T(2,128)} broadcast(bf16[128,2048]{1,0:T(8,128)(2,1)S(1)} %copy-done.3), dimensions={0,2} | broadcast | bytes 2621440 | tf_op jit(solution)/shard_map/mul | solution.py:143
  27.6 3.7 %mul.156 = f32[256,2048]{1,0:T(8,128)} reshape(f32[128,2,2048]{2,1,0:T(2,128)} %mul.155) | data formatting | bytes 4194304 | tf_op jit(solution)/shard_map/mul | solution.py:143
  31.8 4.6 %scatter_custom_fusion.1 = bf16[384,2048]{1,0:T(8,128)(2,1)} fusion(s32[256]{0:T(256)S(1)} %bitcast.93, f32[256,2048]{1,0:T(8,128)} %mul.156, f32[256]{0:T(256)S(1)} %div.42, bf16[]{:T(256)} %constant.16.clone.1), kind=kCustom, calls=%fused_computation.30 | custom fusion | flops 1048576 | bytes 3671042 | tf_op jit(solution)/shard_map/scatter | solution.py:58
  36.4 10.1 %all-to-all-done = bf16[16,24,2048]{2,1,0:T(8,128)(2,1)S(1)} async-done(((bf16[16,24,2048]{2,1,0:T(8,128)(2,1)}), bf16[16,24,2048]{2,1,0:T(8,128)(2,1)S(1)}, u32[]{:S(2)}, u32[]{:S(2)}) %all-to-all-start) | async-done | bytes 1572896 | tf_op jit(solution)/shard_map/all_to_all | solution.py:123
  46.5 6.3 %all-to-all-start.2 = ((bf16[16,24,2048]{2,1,0:T(8,128)(2,1)}), bf16[16,24,2048]{2,1,0:T(8,128)(2,1)S(1)}, u32[]{:S(2)}, u32[]{:S(2)}) async-start(bf16[16,24,2048]{2,1,0:T(8,128)(2,1)} %bitcast.88), calls=%async_computation.2 | async-start | bytes 3145728 | tf_op jit(solution)/shard_map/all_to_all | solution.py:145
  53.0 20.6 %all-gather.2.cloned.1.call-done = bf16[3,2048,768]{2,1,0:T(8,128)(2,1)} async-done(((bf16[3,128,768]{2,1,0:T(8,128)(2,1)}), bf16[3,2048,768]{2,1,0:T(8,128)(2,1)}) %all-gather.2.cloned.1.call-update) | async-done | bytes 9437200 | tf_op jit(solution)/shard_map/all_gather | solution.py:118
  73.6 4.3 %fusion.2 = f32[384,768]{1,0:T(8,128)} fusion(bf16[384,2048]{1,0:T(8,128)(2,1)S(1)} %bitcast.82, bf16[3,2048,768]{2,1,0:T(8,128)(2,1)} %all-gather.2.cloned.1.call-done), kind=kOutput, calls=%fused_computation.12 | convolution fusion | flops 1207959552 | bytes 5898240 | tf_op jit(solution)/shard_map/dot_general | solution.py:62
  77.9 4.3 %fusion.3 = f32[384,768]{1,0:T(8,128)} fusion(bf16[384,2048]{1,0:T(8,128)(2,1)S(1)} %bitcast.83, bf16[3,2048,768]{2,1,0:T(8,128)(2,1)} %all-gather.2.cloned.1.call-done), kind=kOutput, calls=%fused_computation.13 | convolution fusion | flops 1207959552 | bytes 5898240 | tf_op jit(solution)/shard_map/dot_general | solution.py:63
  82.2 4.2 %multiply_convert_fusion.1 = (bf16[384,768]{1,0:T(8,128)(2,1)S(1)}, bf16[384,768]{1,0:T(8,128)(2,1)S(1)}, bf16[384,768]{1,0:T(8,128)(2,1)S(1)}) fusion(f32[384,768]{1,0:T(8,128)} %fusion.2, f32[384,768]{1,0:T(8,128)} %fusion.3, bf16[384,2048]{1,0:T(8,128)(2,1)S(1)} %bitcast.86, bf16[3,2048,768]{2,1,0:T(8,128)(2,1)} %all-gather.2.cloned.1.call-done), kind=kOutput, calls=%fused_computation.21 | convolution fusion | flops 1212678144 | bytes 8847360 | tf_op jit(solution)/shard_map/dot_general | solution.py:72
  92.0 4.6 %fusion = bf16[2048,2304]{1,0:T(8,128)(2,1)} fusion(f32[2048,768]{1,0:T(8,128)S(1)} %fusion.24, f32[2048,768]{1,0:T(8,128)S(1)} %fusion.23, f32[2048,768]{1,0:T(8,128)S(1)} %fusion.22), kind=kLoop, calls=%fused_computation.5 | loop fusion | flops 18874368 | bytes 28311552 | tf_op jit(solution)/shard_map/convert_element_type | solution.py:169
  97.8 4.5 %convolution_convert_fusion = bf16[384,2048]{1,0:T(8,128)(2,1)} fusion(bf16[384,768]{1,0:T(8,128)(2,1)S(1)} %copy-done.10, bf16[3,2048,768]{2,1,0:T(8,128)(2,1)} %all-gather.2.cloned.1.call-done), kind=kOutput, calls=%fused_computation.10 | convolution fusion | flops 1208745984 | bytes 5308416 | tf_op jit(solution)/shard_map/dot_general | solution.py:65
  102.3 7.4 %all-to-all-start.1 = ((bf16[16,24,2048]{2,1,0:T(8,128)(2,1)}), bf16[16,24,2048]{2,1,0:T(8,128)(2,1)S(1)}, u32[]{:S(2)}, u32[]{:S(2)}) async-start(bf16[16,24,2048]{2,1,0:T(8,128)(2,1)} %bitcast.90), calls=%async_computation.1 | async-start | bytes 3145728 | tf_op jit(solution)/shard_map/all_to_all | solution.py:136
  111.3 5.1 %fusion.1 = f32[384,2048]{1,0:T(8,128)} fusion(bf16[384,768]{1,0:T(8,128)(2,1)S(1)} %copy-done.8, bf16[3,2048,768]{2,1,0:T(8,128)(2,1)} %all-gather.2.cloned.1.call-done), kind=kOutput, calls=%fused_computation.11 | convolution fusion | flops 1207959552 | bytes 6881280 | tf_op jit(solution)/shard_map/dot_general | solution.py:77
  116.3 15.2 %all-to-all-done.1 = bf16[16,24,2048]{2,1,0:T(8,128)(2,1)S(1)} async-done(((bf16[16,24,2048]{2,1,0:T(8,128)(2,1)}), bf16[16,24,2048]{2,1,0:T(8,128)(2,1)S(1)}, u32[]{:S(2)}, u32[]{:S(2)}) %all-to-all-start.1) | async-done | bytes 1572896 | tf_op jit(solution)/shard_map/all_to_all | solution.py:136
  131.5 2.4 %gather_fusion = bf16[256,2048]{1,0:T(8,128)(2,1)} fusion(bf16[384,2048]{1,0:T(8,128)(2,1)S(1)} %bitcast.81, s32[1024]{0:T(1024)S(1)} %pad_clamp_fusion), kind=kCustom, calls=%fused_computation | custom fusion | bytes 2098176 | tf_op jit(solution)/shard_map/gather | solution.py:139
  133.9 2.4 %reshape.213 = f32[128,2,2048]{2,1,0:T(2,128)S(1)} reshape(bf16[256,2048]{1,0:T(8,128)(2,1)} %gather_fusion) | data formatting | bytes 3145728 | tf_op jit(solution)/shard_map/convert_element_type | solution.py:139
  136.3 6.0 %multiply_reduce_fusion = (f32[128,2]{1,0:T(8,128)S(1)}, bf16[128,2048]{1,0:T(8,128)(2,1)}) fusion(f32[128,2,2048]{2,1,0:T(2,128)S(1)} %reshape.213, f32[128,2048]{1,0:T(8,128)} %convert_element_type.54, f32[128,2]{1,0:T(8,128)S(1)} %copy.38), kind=kLoop, calls=%fused_computation.18 | loop fusion | flops 1834752 | bytes 3672064 | tf_op jit(solution)/shard_map/reduce_sum | solution.py:142
  143.4 6.3 %all-to-all-start.4 = ((f32[16,128,16]{1,2,0:T(8,128)}), f32[16,128,16]{1,2,0:T(8,128)S(1)}, u32[]{:S(2)}, u32[]{:S(2)}) async-start(f32[16,128,16]{1,2,0:T(8,128)} %bitcast.79), calls=%async_computation.4 | async-start | bytes 262144 | tf_op jit(solution)/shard_map/all_to_all | solution.py:23
  149.7 5.6 %add_convert_fusion = bf16[384,2048]{1,0:T(8,128)(2,1)} fusion(f32[384,2048]{1,0:T(8,128)} %fusion.1, bf16[384,768]{1,0:T(8,128)(2,1)S(1)} %copy-done.6, bf16[3,2048,768]{2,1,0:T(8,128)(2,1)} %all-gather.2.cloned.1.call-done), kind=kOutput, calls=%fused_computation.9 | convolution fusion | flops 1209532416 | bytes 8454144 | tf_op jit(solution)/shard_map/dot_general | solution.py:78
  156.1 6.6 %all-to-all-start.3 = ((bf16[16,24,2048]{2,1,0:T(8,128)(2,1)}), bf16[16,24,2048]{2,1,0:T(8,128)(2,1)S(1)}, u32[]{:S(2)}, u32[]{:S(2)}) async-start(bf16[16,24,2048]{2,1,0:T(8,128)(2,1)} %bitcast.89), calls=%async_computation.3 | async-start | bytes 3145728 | tf_op jit(solution)/shard_map/all_to_all | solution.py:159
  164.0 3.6 %collective-permute-done.1 = f32[128,16]{0,1:T(8,128)S(1)} collective-permute-done((f32[128,16]{0,1:T(8,128)S(1)}, f32[128,16]{0,1:T(8,128)S(1)}, u32[]{:S(2)}, u32[]{:S(2)}) %collective-permute-start.1) | collective-permute-done | bytes 8224 | tf_op jit(solution)/shard_map/ppermute | solution.py:9
  169.0 3.2 %collective-permute-done.2 = f32[128,16]{0,1:T(8,128)S(1)} collective-permute-done((f32[128,16]{0,1:T(8,128)S(1)}, f32[128,16]{0,1:T(8,128)S(1)}, u32[]{:S(2)}, u32[]{:S(2)}) %collective-permute-start.2) | collective-permute-done | bytes 8224 | tf_op jit(solution)/shard_map/ppermute | solution.py:9
  172.2 3.0 %collective-permute-start.3 = (f32[128,16]{0,1:T(8,128)S(1)}, f32[128,16]{0,1:T(8,128)S(1)}, u32[]{:S(2)}, u32[]{:S(2)}) collective-permute-start(f32[128,16]{0,1:T(8,128)S(1)} %add.87), channel_id=1, source_target_pairs={{0,128},{16,144},{32,160},{48,176},{64,192},{80,208},{96,224},{112... | collective-permute-start | bytes 24584 | tf_op jit(solution)/shard_map/ppermute | solution.py:9
  178.4 3.9 %all-to-all-done.3 = bf16[16,24,2048]{2,1,0:T(8,128)(2,1)S(1)} async-done(((bf16[16,24,2048]{2,1,0:T(8,128)(2,1)}), bf16[16,24,2048]{2,1,0:T(8,128)(2,1)S(1)}, u32[]{:S(2)}, u32[]{:S(2)}) %all-to-all-start.3) | async-done | bytes 1572896 | tf_op jit(solution)/shard_map/all_to_all | solution.py:159
  182.3 2.3 %gather_fusion.1 = bf16[256,2048]{1,0:T(8,128)(2,1)} fusion(bf16[384,2048]{1,0:T(8,128)(2,1)S(1)} %bitcast.80, s32[1024]{0:T(1024)S(1)} %pad_clamp_fusion), kind=kCustom, calls=%fused_computation.1 | custom fusion | bytes 2098176 | tf_op jit(solution)/shard_map/gather | solution.py:162
  184.6 2.4 %reshape.214 = f32[128,2,2048]{2,1,0:T(2,128)S(1)} reshape(bf16[256,2048]{1,0:T(8,128)(2,1)} %gather_fusion.1) | data formatting | bytes 3145728 | tf_op jit(solution)/shard_map/convert_element_type | solution.py:162
  187.0 2.8 %reduce_sum.118 = f32[128,2048]{1,0:T(8,128)S(1)} reduce(f32[128,2,2048]{2,1,0:T(2,128)S(1)} %reshape.214, f32[]{:T(128)} %constant.15.clone.1), dimensions={1}, to_apply=%region_9.10 | reduce | flops 262144 | bytes 3145732 | tf_op jit(solution)/shard_map/reduce_sum | solution.py:162
  197.3 6.5 %all-to-all-start.5 = ((f32[16,128,16]{1,2,0:T(8,128)}), f32[16,128,16]{1,2,0:T(8,128)S(1)}, u32[]{:S(2)}, u32[]{:S(2)}) async-start(f32[16,128,16]{1,2,0:T(8,128)} %broadcast_in_dim.19), calls=%async_computation.6 | async-start | bytes 262144 | tf_op jit(solution)/shard_map/all_to_all | solution.py:15
  205.0 16.1 %all-to-all-done.5 = f32[16,128,16]{1,2,0:T(8,128)S(1)} async-done(((f32[16,128,16]{1,2,0:T(8,128)}), f32[16,128,16]{1,2,0:T(8,128)S(1)}, u32[]{:S(2)}, u32[]{:S(2)}) %all-to-all-start.5) | async-done | bytes 131104 | tf_op jit(solution)/shard_map/all_to_all | solution.py:15
  (99 shorter events, 28.4 us)
Async XLA Ops:
  7.2 24.1 %copy-start = (bf16[2048,16]{0,1:T(8,128)(2,1)S(1)}, bf16[2048,16]{0,1:T(8,128)(2,1)}, u32[]{:S(2)}) copy-start(bf16[2048,16]{0,1:T(8,128)(2,1)} %param.12) | copy-start | bytes 196612
  7.2 4.4 %copy-start.1 = (bf16[128,2048]{1,0:T(8,128)(2,1)S(1)}, bf16[128,2048]{1,0:T(8,128)(2,1)}, u32[]{:S(2)}) copy-start(bf16[128,2048]{1,0:T(8,128)(2,1)} %param.8) | copy-start | bytes 1572868
  7.2 66.4 %all-gather.2.cloned.1.call-start = ((), (), s32[]{:S(2)}) async-start(), calls=%async_computation.7 | async-start | bytes 10027008 | tf_op jit(solution)/shard_map/all_gather | solution.py:118
  13.5 11.6 %copy-start.3 = (bf16[128,2048]{1,0:T(8,128)(2,1)S(1)}, bf16[128,2048]{1,0:T(8,128)(2,1)}, u32[]{:S(2)}) copy-start(bf16[128,2048]{1,0:T(8,128)(2,1)} %param.9) | copy-start | bytes 1572868
  17.6 28.9 %all-to-all-start = ((bf16[16,24,2048]{2,1,0:T(8,128)(2,1)}), bf16[16,24,2048]{2,1,0:T(8,128)(2,1)S(1)}, u32[]{:S(2)}, u32[]{:S(2)}) async-start(bf16[16,24,2048]{2,1,0:T(8,128)(2,1)} %bitcast.3), calls=%async_computation | async-start | bytes 3145728 | tf_op jit(solution)/shard_map/all_to_all | solution.py:123
  27.6 3.9 %copy-start.11 = (s32[128,2]{0,1:T(2,128)S(1)}, s32[128,2]{0,1:T(2,128)}, u32[]{:S(2)}) copy-start(s32[128,2]{0,1:T(2,128)} %param.10) | copy-start | bytes 3076
  46.5 35.7 %all-to-all-start.2 = ((bf16[16,24,2048]{2,1,0:T(8,128)(2,1)}), bf16[16,24,2048]{2,1,0:T(8,128)(2,1)S(1)}, u32[]{:S(2)}, u32[]{:S(2)}) async-start(bf16[16,24,2048]{2,1,0:T(8,128)(2,1)} %bitcast.88), calls=%async_computation.2 | async-start | bytes 3145728 | tf_op jit(solution)/shard_map/all_to_all | solution.py:145
  52.8 137.0 %reduce-scatter.2.cloned.1.call-start = ((), (), s32[]{:S(2)}) async-start(), calls=%async_computation.8 | async-start | bytes 10027008 | tf_op jit(solution)/shard_map/reduce_scatter | solution.py:168
  86.4 1.9 copy-start.9
  86.4 1.9 copy-start.5
  86.4 3.7 %copy-start.7 = (bf16[384,768]{1,0:T(8,128)(2,1)}, bf16[384,768]{1,0:T(8,128)(2,1)S(1)}, u32[]{:S(2)}) copy-start(bf16[384,768]{1,0:T(8,128)(2,1)S(1)} %get-tuple-element.25) | copy-start | bytes 1769476
  96.7 1.1 copy-start.10
  102.3 7.6 %copy-start.4 = (bf16[128,2048]{1,0:T(8,128)(2,1)S(1)}, bf16[128,2048]{1,0:T(8,128)(2,1)}, u32[]{:S(2)}) copy-start(bf16[128,2048]{1,0:T(8,128)(2,1)} %param.9) | copy-start | bytes 1572868
  102.3 9.0 %copy-start.8 = (bf16[384,768]{1,0:T(8,128)(2,1)S(1)}, bf16[384,768]{1,0:T(8,128)(2,1)}, u32[]{:S(2)}) copy-start(bf16[384,768]{1,0:T(8,128)(2,1)} %copy-done.7) | copy-start | bytes 1769476
  102.3 29.2 %all-to-all-start.1 = ((bf16[16,24,2048]{2,1,0:T(8,128)(2,1)}), bf16[16,24,2048]{2,1,0:T(8,128)(2,1)S(1)}, u32[]{:S(2)}, u32[]{:S(2)}) async-start(bf16[16,24,2048]{2,1,0:T(8,128)(2,1)} %bitcast.90), calls=%async_computation.1 | async-start | bytes 3145728 | tf_op jit(solution)/shard_map/all_to_all | solution.py:136
  136.3 6.2 %copy-start.2 = (bf16[128,2048]{1,0:T(8,128)(2,1)S(1)}, bf16[128,2048]{1,0:T(8,128)(2,1)}, u32[]{:S(2)}) copy-start(bf16[128,2048]{1,0:T(8,128)(2,1)} %param.8) | copy-start | bytes 1572868
  136.3 13.4 %copy-start.6 = (bf16[384,768]{1,0:T(8,128)(2,1)S(1)}, bf16[384,768]{1,0:T(8,128)(2,1)}, u32[]{:S(2)}) copy-start(bf16[384,768]{1,0:T(8,128)(2,1)} %copy-done.5) | copy-start | bytes 1769476
  143.4 12.7 %all-to-all-start.4 = ((f32[16,128,16]{1,2,0:T(8,128)}), f32[16,128,16]{1,2,0:T(8,128)S(1)}, u32[]{:S(2)}, u32[]{:S(2)}) async-start(f32[16,128,16]{1,2,0:T(8,128)} %bitcast.79), calls=%async_computation.4 | async-start | bytes 262144 | tf_op jit(solution)/shard_map/all_to_all | solution.py:23
  155.3 19.9 %copy-start.12 = (s32[16]{0:T(128)S(1)}, s32[16]{0:T(128)}, u32[]{:S(2)}) copy-start(s32[16]{0:T(128)} %param.11) | copy-start | bytes 196
  156.1 26.2 %all-to-all-start.3 = ((bf16[16,24,2048]{2,1,0:T(8,128)(2,1)}), bf16[16,24,2048]{2,1,0:T(8,128)(2,1)S(1)}, u32[]{:S(2)}, u32[]{:S(2)}) async-start(bf16[16,24,2048]{2,1,0:T(8,128)(2,1)} %bitcast.89), calls=%async_computation.3 | async-start | bytes 3145728 | tf_op jit(solution)/shard_map/all_to_all | solution.py:159
  162.7 1.3 collective-permute-start
  164.0 3.7 %collective-permute-start.1 = (f32[128,16]{0,1:T(8,128)S(1)}, f32[128,16]{0,1:T(8,128)S(1)}, u32[]{:S(2)}, u32[]{:S(2)}) collective-permute-start(f32[128,16]{0,1:T(8,128)S(1)} %add.85), channel_id=1, source_target_pairs={{0,32},{16,48},{32,0},{48,16},{64,96},{80,112},{96,64},{112,80},{1... | collective-permute-start | bytes 24584 | tf_op jit(solution)/shard_map/ppermute | solution.py:9
  167.6 4.5 %collective-permute-start.2 = (f32[128,16]{0,1:T(8,128)S(1)}, f32[128,16]{0,1:T(8,128)S(1)}, u32[]{:S(2)}, u32[]{:S(2)}) collective-permute-start(f32[128,16]{0,1:T(8,128)S(1)} %add.86), channel_id=1, source_target_pairs={{0,64},{16,80},{32,96},{48,112},{64,0},{80,16},{96,32},{112,48},{1... | collective-permute-start | bytes 24584 | tf_op jit(solution)/shard_map/ppermute | solution.py:9
  172.2 17.6 %collective-permute-start.3 = (f32[128,16]{0,1:T(8,128)S(1)}, f32[128,16]{0,1:T(8,128)S(1)}, u32[]{:S(2)}, u32[]{:S(2)}) collective-permute-start(f32[128,16]{0,1:T(8,128)S(1)} %add.87), channel_id=1, source_target_pairs={{0,128},{16,144},{32,160},{48,176},{64,192},{80,208},{96,224},{112... | collective-permute-start | bytes 24584 | tf_op jit(solution)/shard_map/ppermute | solution.py:9
  191.1 30.7 %collective-permute-start.4 = (bf16[3,128,768]{2,1,0:T(8,128)(2,1)S(1)}, bf16[3,128,768]{2,1,0:T(8,128)(2,1)S(1)}, u32[]{:S(2)}, u32[]{:S(2)}) collective-permute-start(bf16[3,128,768]{2,1,0:T(8,128)(2,1)S(1)} %pad_maximum_fusion.1), channel_id=1, source_target_pairs={{0,1},{1,0},{2,3},{3,2},{4,5},{5,4},{6,7},{7,6},{8,9},{9,8},{10,11... | collective-permute-start | bytes 1769480 | tf_op jit(solution)/shard_map/ppermute | solution.py:9
  191.7 30.1 %collective-permute-start.5 = (bf16[3,128,768]{2,1,0:T(8,128)(2,1)S(1)}, bf16[3,128,768]{2,1,0:T(8,128)(2,1)S(1)}, u32[]{:S(2)}, u32[]{:S(2)}) collective-permute-start(bf16[3,128,768]{2,1,0:T(8,128)(2,1)S(1)} %pad_maximum_fusion.1), channel_id=1, source_target_pairs={{0,2},{1,3},{2,0},{3,1},{4,6},{5,7},{6,4},{7,5},{8,10},{9,11},{10,... | collective-permute-start | bytes 1769480 | tf_op jit(solution)/shard_map/ppermute | solution.py:9
  193.7 28.1 %collective-permute-start.6 = (bf16[3,128,768]{2,1,0:T(8,128)(2,1)S(1)}, bf16[3,128,768]{2,1,0:T(8,128)(2,1)}, u32[]{:S(2)}, u32[]{:S(2)}) collective-permute-start(bf16[3,128,768]{2,1,0:T(8,128)(2,1)S(1)} %pad_maximum_fusion.1), channel_id=1, source_target_pairs={{0,4},{1,5},{2,6},{3,7},{4,0},{5,1},{6,2},{7,3},{8,12},{9,13},{10,... | collective-permute-start | bytes 1769480 | tf_op jit(solution)/shard_map/ppermute | solution.py:9
  195.7 26.1 %collective-permute-start.7 = (bf16[3,128,768]{2,1,0:T(8,128)(2,1)S(1)}, bf16[3,128,768]{2,1,0:T(8,128)(2,1)}, u32[]{:S(2)}, u32[]{:S(2)}) collective-permute-start(bf16[3,128,768]{2,1,0:T(8,128)(2,1)S(1)} %pad_maximum_fusion.1), channel_id=1, source_target_pairs={{0,8},{1,9},{2,10},{3,11},{4,12},{5,13},{6,14},{7,15},{8,0},{9,1},... | collective-permute-start | bytes 1769480 | tf_op jit(solution)/shard_map/ppermute | solution.py:9
  197.3 23.8 %all-to-all-start.5 = ((f32[16,128,16]{1,2,0:T(8,128)}), f32[16,128,16]{1,2,0:T(8,128)S(1)}, u32[]{:S(2)}, u32[]{:S(2)}) async-start(f32[16,128,16]{1,2,0:T(8,128)} %broadcast_in_dim.19), calls=%async_computation.6 | async-start | bytes 262144 | tf_op jit(solution)/shard_map/all_to_all | solution.py:15
Sparse Core Ops, SparseCore 0:
  9.9 63.7 all-gather.1
  96.8 71.8 reduce-scatter.1

commit v2 on v0

--- a/solution.py
+++ b/solution.py
@@ -29,9 +29,13 @@
     for bit_level in range(replicas.bit_length() - 1):
         piece = piece + swapped(piece, "dp", bit_level)
     piece, arrivals = lax.optimization_barrier((piece, arrivals))
-    chosen = companion
-    for bit_level, arrived in enumerate(arrivals):
-        chosen = jnp.where(partner == jnp.bitwise_xor(my_index, 1 << bit_level), arrived, chosen)
+    chosen = []
+    for index in range(companion.shape[0]):
+        own = companion[index : index + 1]
+        for bit_level, arrived in enumerate(arrivals):
+            mate = partner == jnp.bitwise_xor(my_index, 1 << bit_level)
+            own = jnp.where(mate, arrived[index : index + 1], own)
+        chosen.append(own)
     return gather_by_exchange(piece, "expert"), chosen
 
 
@@ -181,7 +185,7 @@
         d_logits, router_weight, (((1,), (1,)), ((), ())), preferred_element_type=jnp.float32
     )
     token_grad = (d_expert + router_back).astype(jnp.bfloat16)
-    return (mixed, token_grad, grad_stack[0:1], grad_stack[1:2], grad_stack[2:3], router_grad)
+    return (mixed, token_grad, grad_stack[0], grad_stack[1], grad_stack[2], router_grad)
 
 
 def solution(mesh):

time: 227 us -> 227 us (level)
  no operation moved by 1% of the time
where the time goes in v2:
time: 227 us; the launch traced here: 226 us
  waiting for transfers between devices  69.8 us (31%)
  starting transfers between devices  50.1 us (22%)
  matrix products  35 us (15%)
  local copies, waits for them, and re-layouts  27.4 us (12%)
  other arithmetic  27.1 us (12%)
  between operations  17 us (7%)
    all_gather x1, waiting for transfers between devices, on_device(): gathered = lax.all_gather(held, 'dp', axis=1, tiled=True)  20.6 us
    all_to_all x1, waiting for transfers between devices, on_device(): lax.all_to_all(result, 'expert', split_axis=0, concat_axis=0, tiled=True)  15.2 us
    ppermute x8, waiting for transfers between devices, swapped(): lax.ppermute(array, axis, [(i, i ^ 1 << stride) for i in range(lax.axis_s...  13.5 us
    ppermute x8, starting transfers between devices, swapped(): lax.ppermute(array, axis, [(i, i ^ 1 << stride) for i in range(lax.axis_s...  10.9 us
    all_to_all x1, waiting for transfers between devices, on_device(): lax.all_to_all(outbox, 'expert', split_axis=0, concat_axis=0, tiled=True)  10.1 us
    all_to_all x1, starting transfers between devices, on_device(): lax.all_to_all(outbox, 'expert', split_axis=0, concat_axis=0, tiled=True)  7.48 us
    all_to_all x1, starting transfers between devices, on_device(): lax.all_to_all(result, 'expert', split_axis=0, concat_axis=0, tiled=True)  7.41 us
    all_to_all x1, starting transfers between devices, on_device(): lax.all_to_all(d_rows.reshape(groups, capacity, width), 'expert', split_a...  6.59 us
  transfers between devices with their start and end apart: 16, of which 11 were waited for; matrix products, arithmetic and copies ran while one was open for 31% of the time, Pallas kernels for 0%

profile of v2, /device:TPU:2, one launch (start us, length us, event | category | flops | bytes accessed | tf_op | source)
XLA Modules:
  0.0 226.4 jit_solution(8632716784948537839)
XLA Ops:
  13.5 4.1 %scatter_custom_fusion = bf16[384,2048]{1,0:T(8,128)(2,1)} fusion(s32[256]{0:T(256)S(1)} %bitcast.92, bf16[256,2048]{1,0:T(8,128)(2,1)} %reshape.199, bf16[]{:T(256)} %constant.16.clone.1), kind=kCustom, calls=%fused_computation.33 | custom fusion | bytes 1573376 | tf_op jit(solution)/shard_map/scatter | solution.py:61
  17.6 7.5 %all-to-all-start = ((bf16[16,24,2048]{2,1,0:T(8,128)(2,1)}), bf16[16,24,2048]{2,1,0:T(8,128)(2,1)S(1)}, u32[]{:S(2)}, u32[]{:S(2)}) async-start(bf16[16,24,2048]{2,1,0:T(8,128)(2,1)} %bitcast.3), calls=%async_computation | async-start | bytes 3145728 | tf_op jit(solution)/shard_map/all_to_all | solution.py:126
  25.1 2.5 %mul.155 = f32[128,2,2048]{2,1,0:T(2,128)} broadcast(bf16[128,2048]{1,0:T(8,128)(2,1)S(1)} %copy-done.3), dimensions={0,2} | broadcast | bytes 2621440 | tf_op jit(solution)/shard_map/mul | solution.py:146
  27.6 3.7 %mul.156 = f32[256,2048]{1,0:T(8,128)} reshape(f32[128,2,2048]{2,1,0:T(2,128)} %mul.155) | data formatting | bytes 4194304 | tf_op jit(solution)/shard_map/mul | solution.py:146
  31.8 4.6 %scatter_custom_fusion.1 = bf16[384,2048]{1,0:T(8,128)(2,1)} fusion(s32[256]{0:T(256)S(1)} %bitcast.93, f32[256,2048]{1,0:T(8,128)} %mul.156, f32[256]{0:T(256)S(1)} %div.42, bf16[]{:T(256)} %constant.16.clone.1), kind=kCustom, calls=%fused_computation.30 | custom fusion | flops 1048576 | bytes 3671042 | tf_op jit(solution)/shard_map/scatter | solution.py:61
  36.4 10.1 %all-to-all-done = bf16[16,24,2048]{2,1,0:T(8,128)(2,1)S(1)} async-done(((bf16[16,24,2048]{2,1,0:T(8,128)(2,1)}), bf16[16,24,2048]{2,1,0:T(8,128)(2,1)S(1)}, u32[]{:S(2)}, u32[]{:S(2)}) %all-to-all-start) | async-done | bytes 1572896 | tf_op jit(solution)/shard_map/all_to_all | solution.py:126
  46.5 6.3 %all-to-all-start.2 = ((bf16[16,24,2048]{2,1,0:T(8,128)(2,1)}), bf16[16,24,2048]{2,1,0:T(8,128)(2,1)S(1)}, u32[]{:S(2)}, u32[]{:S(2)}) async-start(bf16[16,24,2048]{2,1,0:T(8,128)(2,1)} %bitcast.88), calls=%async_computation.2 | async-start | bytes 3145728 | tf_op jit(solution)/shard_map/all_to_all | solution.py:148
  53.0 20.6 %all-gather.2.cloned.1.call-done = bf16[3,2048,768]{2,1,0:T(8,128)(2,1)} async-done(((bf16[3,128,768]{2,1,0:T(8,128)(2,1)}), bf16[3,2048,768]{2,1,0:T(8,128)(2,1)}) %all-gather.2.cloned.1.call-update) | async-done | bytes 9437200 | tf_op jit(solution)/shard_map/all_gather | solution.py:121
  73.6 4.3 %fusion.2 = f32[384,768]{1,0:T(8,128)} fusion(bf16[384,2048]{1,0:T(8,128)(2,1)S(1)} %bitcast.82, bf16[3,2048,768]{2,1,0:T(8,128)(2,1)} %all-gather.2.cloned.1.call-done), kind=kOutput, calls=%fused_computation.12 | convolution fusion | flops 1207959552 | bytes 5898240 | tf_op jit(solution)/shard_map/dot_general | solution.py:65
  77.9 4.3 %fusion.3 = f32[384,768]{1,0:T(8,128)} fusion(bf16[384,2048]{1,0:T(8,128)(2,1)S(1)} %bitcast.83, bf16[3,2048,768]{2,1,0:T(8,128)(2,1)} %all-gather.2.cloned.1.call-done), kind=kOutput, calls=%fused_computation.13 | convolution fusion | flops 1207959552 | bytes 5898240 | tf_op jit(solution)/shard_map/dot_general | solution.py:66
  82.2 4.2 %multiply_convert_fusion.1 = (bf16[384,768]{1,0:T(8,128)(2,1)S(1)}, bf16[384,768]{1,0:T(8,128)(2,1)S(1)}, bf16[384,768]{1,0:T(8,128)(2,1)S(1)}) fusion(f32[384,768]{1,0:T(8,128)} %fusion.2, f32[384,768]{1,0:T(8,128)} %fusion.3, bf16[384,2048]{1,0:T(8,128)(2,1)S(1)} %bitcast.86, bf16[3,2048,768]{2,1,0:T(8,128)(2,1)} %all-gather.2.cloned.1.call-done), kind=kOutput, calls=%fused_computation.21 | convolution fusion | flops 1212678144 | bytes 8847360 | tf_op jit(solution)/shard_map/dot_general | solution.py:75
  92.0 4.6 %fusion = bf16[2048,2304]{1,0:T(8,128)(2,1)} fusion(f32[2048,768]{1,0:T(8,128)S(1)} %fusion.23, f32[2048,768]{1,0:T(8,128)S(1)} %fusion.22, f32[2048,768]{1,0:T(8,128)S(1)} %fusion.21), kind=kLoop, calls=%fused_computation.5 | loop fusion | flops 18874368 | bytes 28311552 | tf_op jit(solution)/shard_map/convert_element_type | solution.py:172
  97.8 4.5 %convolution_convert_fusion = bf16[384,2048]{1,0:T(8,128)(2,1)} fusion(bf16[384,768]{1,0:T(8,128)(2,1)S(1)} %copy-done.10, bf16[3,2048,768]{2,1,0:T(8,128)(2,1)} %all-gather.2.cloned.1.call-done), kind=kOutput, calls=%fused_computation.10 | convolution fusion | flops 1208745984 | bytes 5308416 | tf_op jit(solution)/shard_map/dot_general | solution.py:68
  102.3 7.4 %all-to-all-start.1 = ((bf16[16,24,2048]{2,1,0:T(8,128)(2,1)}), bf16[16,24,2048]{2,1,0:T(8,128)(2,1)S(1)}, u32[]{:S(2)}, u32[]{:S(2)}) async-start(bf16[16,24,2048]{2,1,0:T(8,128)(2,1)} %bitcast.90), calls=%async_computation.1 | async-start | bytes 3145728 | tf_op jit(solution)/shard_map/all_to_all | solution.py:139
  111.3 5.1 %fusion.1 = f32[384,2048]{1,0:T(8,128)} fusion(bf16[384,768]{1,0:T(8,128)(2,1)S(1)} %copy-done.8, bf16[3,2048,768]{2,1,0:T(8,128)(2,1)} %all-gather.2.cloned.1.call-done), kind=kOutput, calls=%fused_computation.11 | convolution fusion | flops 1207959552 | bytes 6881280 | tf_op jit(solution)/shard_map/dot_general | solution.py:80
  116.3 15.2 %all-to-all-done.1 = bf16[16,24,2048]{2,1,0:T(8,128)(2,1)S(1)} async-done(((bf16[16,24,2048]{2,1,0:T(8,128)(2,1)}), bf16[16,24,2048]{2,1,0:T(8,128)(2,1)S(1)}, u32[]{:S(2)}, u32[]{:S(2)}) %all-to-all-start.1) | async-done | bytes 1572896 | tf_op jit(solution)/shard_map/all_to_all | solution.py:139
  131.5 2.4 %gather_fusion = bf16[256,2048]{1,0:T(8,128)(2,1)} fusion(bf16[384,2048]{1,0:T(8,128)(2,1)S(1)} %bitcast.81, s32[1024]{0:T(1024)S(1)} %pad_clamp_fusion), kind=kCustom, calls=%fused_computation | custom fusion | bytes 2098176 | tf_op jit(solution)/shard_map/gather | solution.py:142
  133.9 2.4 %reshape.213 = f32[128,2,2048]{2,1,0:T(2,128)S(1)} reshape(bf16[256,2048]{1,0:T(8,128)(2,1)} %gather_fusion) | data formatting | bytes 3145728 | tf_op jit(solution)/shard_map/convert_element_type | solution.py:142
  136.3 6.0 %multiply_reduce_fusion = (f32[128,2]{1,0:T(8,128)S(1)}, bf16[128,2048]{1,0:T(8,128)(2,1)}) fusion(f32[128,2,2048]{2,1,0:T(2,128)S(1)} %reshape.213, f32[128,2048]{1,0:T(8,128)} %convert_element_type.54, f32[128,2]{1,0:T(8,128)S(1)} %copy.38), kind=kLoop, calls=%fused_computation.18 | loop fusion | flops 1834752 | bytes 3672064 | tf_op jit(solution)/shard_map/reduce_sum | solution.py:145
  143.4 6.3 %all-to-all-start.4 = ((f32[16,128,16]{1,2,0:T(8,128)}), f32[16,128,16]{1,2,0:T(8,128)S(1)}, u32[]{:S(2)}, u32[]{:S(2)}) async-start(f32[16,128,16]{1,2,0:T(8,128)} %bitcast.79), calls=%async_computation.4 | async-start | bytes 262144 | tf_op jit(solution)/shard_map/all_to_all | solution.py:23
  149.7 5.6 %add_convert_fusion = bf16[384,2048]{1,0:T(8,128)(2,1)} fusion(f32[384,2048]{1,0:T(8,128)} %fusion.1, bf16[384,768]{1,0:T(8,128)(2,1)S(1)} %copy-done.6, bf16[3,2048,768]{2,1,0:T(8,128)(2,1)} %all-gather.2.cloned.1.call-done), kind=kOutput, calls=%fused_computation.9 | convolution fusion | flops 1209532416 | bytes 8454144 | tf_op jit(solution)/shard_map/dot_general | solution.py:81
  156.1 6.6 %all-to-all-start.3 = ((bf16[16,24,2048]{2,1,0:T(8,128)(2,1)}), bf16[16,24,2048]{2,1,0:T(8,128)(2,1)S(1)}, u32[]{:S(2)}, u32[]{:S(2)}) async-start(bf16[16,24,2048]{2,1,0:T(8,128)(2,1)} %bitcast.89), calls=%async_computation.3 | async-start | bytes 3145728 | tf_op jit(solution)/shard_map/all_to_all | solution.py:162
  162.7 6.0 %reduce-scatter.2.cloned.1.call-done = bf16[128,2304]{1,0:T(8,128)(2,1)} async-done(((bf16[2048,2304]{1,0:T(8,128)(2,1)}), bf16[128,2304]{1,0:T(8,128)(2,1)}) %reduce-scatter.2.cloned.1.call-update) | async-done | bytes 589840 | tf_op jit(solution)/shard_map/reduce_scatter | solution.py:171
  172.2 2.7 %collective-permute-start.5 = (bf16[3,128,768]{2,1,0:T(8,128)(2,1)}, bf16[3,128,768]{2,1,0:T(8,128)(2,1)}, u32[]{:S(2)}, u32[]{:S(2)}) collective-permute-start(bf16[3,128,768]{2,1,0:T(8,128)(2,1)} %pad_maximum_fusion.1), channel_id=1, source_target_pairs={{0,2},{1,3},{2,0},{3,1},{4,6},{5,7},{6,4},{7,5},{8,10},{9,11},{10,... | collective-permute-start | bytes 1769480 | tf_op jit(solution)/shard_map/ppermute | solution.py:9
  178.9 3.6 %collective-permute-done.1 = f32[128,16]{0,1:T(8,128)S(1)} collective-permute-done((f32[128,16]{0,1:T(8,128)S(1)}, f32[128,16]{0,1:T(8,128)S(1)}, u32[]{:S(2)}, u32[]{:S(2)}) %collective-permute-start.1) | collective-permute-done | bytes 8224 | tf_op jit(solution)/shard_map/ppermute | solution.py:9
  191.6 2.8 %reduce_sum.118 = f32[128,2048]{1,0:T(8,128)S(1)} reduce(f32[128,2,2048]{2,1,0:T(2,128)S(1)} %reshape.214, f32[]{:T(128)} %constant.15.clone.1), dimensions={1}, to_apply=%region_9.10 | reduce | flops 262144 | bytes 3145732 | tf_op jit(solution)/shard_map/reduce_sum | solution.py:165
  194.3 2.9 %collective-permute-start.3 = (f32[128,16]{0,1:T(8,128)S(1)}, f32[128,16]{0,1:T(8,128)S(1)}, u32[]{:S(2)}, u32[]{:S(2)}) collective-permute-start(f32[128,16]{0,1:T(8,128)S(1)} %add.87), channel_id=1, source_target_pairs={{0,128},{16,144},{32,160},{48,176},{64,192},{80,208},{96,224},{112... | collective-permute-start | bytes 24584 | tf_op jit(solution)/shard_map/ppermute | solution.py:9
  198.4 3.6 %collective-permute-done.3 = f32[128,16]{0,1:T(8,128)S(1)} collective-permute-done((f32[128,16]{0,1:T(8,128)S(1)}, f32[128,16]{0,1:T(8,128)S(1)}, u32[]{:S(2)}, u32[]{:S(2)}) %collective-permute-start.3) | collective-permute-done | bytes 8224 | tf_op jit(solution)/shard_map/ppermute | solution.py:9
  202.0 4.4 %collective-permute-done.5 = bf16[3,128,768]{2,1,0:T(8,128)(2,1)} collective-permute-done((bf16[3,128,768]{2,1,0:T(8,128)(2,1)}, bf16[3,128,768]{2,1,0:T(8,128)(2,1)}, u32[]{:S(2)}, u32[]{:S(2)}) %collective-permute-start.5) | collective-permute-done | bytes 589856 | tf_op jit(solution)/shard_map/ppermute | solution.py:9
  207.7 4.8 %all-to-all-start.5 = ((f32[16,128,16]{1,2,0:T(8,128)}), f32[16,128,16]{1,2,0:T(8,128)S(1)}, u32[]{:S(2)}, u32[]{:S(2)}) async-start(f32[16,128,16]{1,2,0:T(8,128)} %broadcast_in_dim.19), calls=%async_computation.6 | async-start | bytes 262144 | tf_op jit(solution)/shard_map/all_to_all | solution.py:15
  212.5 2.7 %select_select_fusion = (bf16[1,128,768]{2,1,0:T(8,128)(2,1)}, bf16[1,128,768]{2,1,0:T(8,128)(2,1)}, bf16[1,128,768]{2,1,0:T(8,128)(2,1)}) fusion(bf16[3,128,768]{2,1,0:T(8,128)(2,1)} %pad_maximum_fusion.1, bf16[3,128,768]{2,1,0:T(8,128)(2,1)} %collective-permute-done.4, bf16[3,128,768]{2,1,0:T(8,128)(2,1)} %collective-permute-done.5, ...), kind=kLoop, calls=%fused_computation.40 | loop fusion | flops 1179648 | bytes 3538948 | tf_op jit(solution)/shard_map/jit(_where)/select_n | solution.py:37
  215.2 3.6 %all-to-all-done.5 = f32[16,128,16]{1,2,0:T(8,128)S(1)} async-done(((f32[16,128,16]{1,2,0:T(8,128)}), f32[16,128,16]{1,2,0:T(8,128)S(1)}, u32[]{:S(2)}, u32[]{:S(2)}) %all-to-all-start.5) | async-done | bytes 131104 | tf_op jit(solution)/shard_map/all_to_all | solution.py:15
  (98 shorter events, 33.9 us)
Async XLA Ops:
  7.2 24.1 %copy-start = (bf16[2048,16]{0,1:T(8,128)(2,1)S(1)}, bf16[2048,16]{0,1:T(8,128)(2,1)}, u32[]{:S(2)}) copy-start(bf16[2048,16]{0,1:T(8,128)(2,1)} %param.12) | copy-start | bytes 196612
  7.2 4.4 %copy-start.1 = (bf16[128,2048]{1,0:T(8,128)(2,1)S(1)}, bf16[128,2048]{1,0:T(8,128)(2,1)}, u32[]{:S(2)}) copy-start(bf16[128,2048]{1,0:T(8,128)(2,1)} %param.8) | copy-start | bytes 1572868
  7.2 66.4 %all-gather.2.cloned.1.call-start = ((), (), s32[]{:S(2)}) async-start(), calls=%async_computation.7 | async-start | bytes 10027008 | tf_op jit(solution)/shard_map/all_gather | solution.py:121
  13.5 11.6 %copy-start.3 = (bf16[128,2048]{1,0:T(8,128)(2,1)S(1)}, bf16[128,2048]{1,0:T(8,128)(2,1)}, u32[]{:S(2)}) copy-start(bf16[128,2048]{1,0:T(8,128)(2,1)} %param.9) | copy-start | bytes 1572868
  17.6 28.9 %all-to-all-start = ((bf16[16,24,2048]{2,1,0:T(8,128)(2,1)}), bf16[16,24,2048]{2,1,0:T(8,128)(2,1)S(1)}, u32[]{:S(2)}, u32[]{:S(2)}) async-start(bf16[16,24,2048]{2,1,0:T(8,128)(2,1)} %bitcast.3), calls=%async_computation | async-start | bytes 3145728 | tf_op jit(solution)/shard_map/all_to_all | solution.py:126
  27.6 3.9 %copy-start.11 = (s32[128,2]{0,1:T(2,128)S(1)}, s32[128,2]{0,1:T(2,128)}, u32[]{:S(2)}) copy-start(s32[128,2]{0,1:T(2,128)} %param.10) | copy-start | bytes 3076
  46.5 35.7 %all-to-all-start.2 = ((bf16[16,24,2048]{2,1,0:T(8,128)(2,1)}), bf16[16,24,2048]{2,1,0:T(8,128)(2,1)S(1)}, u32[]{:S(2)}, u32[]{:S(2)}) async-start(bf16[16,24,2048]{2,1,0:T(8,128)(2,1)} %bitcast.88), calls=%async_computation.2 | async-start | bytes 3145728 | tf_op jit(solution)/shard_map/all_to_all | solution.py:148
  52.8 116.0 %reduce-scatter.2.cloned.1.call-start = ((), (), s32[]{:S(2)}) async-start(), calls=%async_computation.8 | async-start | bytes 10027008 | tf_op jit(solution)/shard_map/reduce_scatter | solution.py:171
  86.4 1.9 copy-start.9
  86.4 1.9 copy-start.5
  86.4 3.7 %copy-start.7 = (bf16[384,768]{1,0:T(8,128)(2,1)}, bf16[384,768]{1,0:T(8,128)(2,1)S(1)}, u32[]{:S(2)}) copy-start(bf16[384,768]{1,0:T(8,128)(2,1)S(1)} %get-tuple-element.28) | copy-start | bytes 1769476
  96.7 1.1 copy-start.10
  102.3 7.6 %copy-start.4 = (bf16[128,2048]{1,0:T(8,128)(2,1)S(1)}, bf16[128,2048]{1,0:T(8,128)(2,1)}, u32[]{:S(2)}) copy-start(bf16[128,2048]{1,0:T(8,128)(2,1)} %param.9) | copy-start | bytes 1572868
  102.3 9.0 %copy-start.8 = (bf16[384,768]{1,0:T(8,128)(2,1)S(1)}, bf16[384,768]{1,0:T(8,128)(2,1)}, u32[]{:S(2)}) copy-start(bf16[384,768]{1,0:T(8,128)(2,1)} %copy-done.7) | copy-start | bytes 1769476
  102.3 29.2 %all-to-all-start.1 = ((bf16[16,24,2048]{2,1,0:T(8,128)(2,1)}), bf16[16,24,2048]{2,1,0:T(8,128)(2,1)S(1)}, u32[]{:S(2)}, u32[]{:S(2)}) async-start(bf16[16,24,2048]{2,1,0:T(8,128)(2,1)} %bitcast.90), calls=%async_computation.1 | async-start | bytes 3145728 | tf_op jit(solution)/shard_map/all_to_all | solution.py:139
  136.3 6.2 %copy-start.2 = (bf16[128,2048]{1,0:T(8,128)(2,1)S(1)}, bf16[128,2048]{1,0:T(8,128)(2,1)}, u32[]{:S(2)}) copy-start(bf16[128,2048]{1,0:T(8,128)(2,1)} %param.8) | copy-start | bytes 1572868
  136.3 13.4 %copy-start.6 = (bf16[384,768]{1,0:T(8,128)(2,1)S(1)}, bf16[384,768]{1,0:T(8,128)(2,1)}, u32[]{:S(2)}) copy-start(bf16[384,768]{1,0:T(8,128)(2,1)} %copy-done.5) | copy-start | bytes 1769476
  143.4 12.7 %all-to-all-start.4 = ((f32[16,128,16]{1,2,0:T(8,128)}), f32[16,128,16]{1,2,0:T(8,128)S(1)}, u32[]{:S(2)}, u32[]{:S(2)}) async-start(f32[16,128,16]{1,2,0:T(8,128)} %bitcast.79), calls=%async_computation.4 | async-start | bytes 262144 | tf_op jit(solution)/shard_map/all_to_all | solution.py:23
  156.1 27.5 %copy-start.12 = (s32[16]{0:T(128)S(1)}, s32[16]{0:T(128)}, u32[]{:S(2)}) copy-start(s32[16]{0:T(128)} %param.11) | copy-start | bytes 196
  156.1 30.7 %all-to-all-start.3 = ((bf16[16,24,2048]{2,1,0:T(8,128)(2,1)}), bf16[16,24,2048]{2,1,0:T(8,128)(2,1)S(1)}, u32[]{:S(2)}, u32[]{:S(2)}) async-start(bf16[16,24,2048]{2,1,0:T(8,128)(2,1)} %bitcast.89), calls=%async_computation.3 | async-start | bytes 3145728 | tf_op jit(solution)/shard_map/all_to_all | solution.py:162
  170.8 31.2 %collective-permute-start.4 = (bf16[3,128,768]{2,1,0:T(8,128)(2,1)}, bf16[3,128,768]{2,1,0:T(8,128)(2,1)}, u32[]{:S(2)}, u32[]{:S(2)}) collective-permute-start(bf16[3,128,768]{2,1,0:T(8,128)(2,1)} %pad_maximum_fusion.1), channel_id=1, source_target_pairs={{0,1},{1,0},{2,3},{3,2},{4,5},{5,4},{6,7},{7,6},{8,9},{9,8},{10,11... | collective-permute-start | bytes 1769480 | tf_op jit(solution)/shard_map/ppermute | solution.py:9
  172.2 34.1 %collective-permute-start.5 = (bf16[3,128,768]{2,1,0:T(8,128)(2,1)}, bf16[3,128,768]{2,1,0:T(8,128)(2,1)}, u32[]{:S(2)}, u32[]{:S(2)}) collective-permute-start(bf16[3,128,768]{2,1,0:T(8,128)(2,1)} %pad_maximum_fusion.1), channel_id=1, source_target_pairs={{0,2},{1,3},{2,0},{3,1},{4,6},{5,7},{6,4},{7,5},{8,10},{9,11},{10,... | collective-permute-start | bytes 1769480 | tf_op jit(solution)/shard_map/ppermute | solution.py:9
  175.0 31.4 %collective-permute-start.6 = (bf16[3,128,768]{2,1,0:T(8,128)(2,1)}, bf16[3,128,768]{2,1,0:T(8,128)(2,1)}, u32[]{:S(2)}, u32[]{:S(2)}) collective-permute-start(bf16[3,128,768]{2,1,0:T(8,128)(2,1)} %pad_maximum_fusion.1), channel_id=1, source_target_pairs={{0,4},{1,5},{2,6},{3,7},{4,0},{5,1},{6,2},{7,3},{8,12},{9,13},{10,... | collective-permute-start | bytes 1769480 | tf_op jit(solution)/shard_map/ppermute | solution.py:9
  175.5 31.5 %collective-permute-start.7 = (bf16[3,128,768]{2,1,0:T(8,128)(2,1)}, bf16[3,128,768]{2,1,0:T(8,128)(2,1)}, u32[]{:S(2)}, u32[]{:S(2)}) collective-permute-start(bf16[3,128,768]{2,1,0:T(8,128)(2,1)} %pad_maximum_fusion.1), channel_id=1, source_target_pairs={{0,8},{1,9},{2,10},{3,11},{4,12},{5,13},{6,14},{7,15},{8,0},{9,1},... | collective-permute-start | bytes 1769480 | tf_op jit(solution)/shard_map/ppermute | solution.py:9
  177.8 1.2 collective-permute-start
  178.9 3.7 %collective-permute-start.1 = (f32[128,16]{0,1:T(8,128)S(1)}, f32[128,16]{0,1:T(8,128)S(1)}, u32[]{:S(2)}, u32[]{:S(2)}) collective-permute-start(f32[128,16]{0,1:T(8,128)S(1)} %add.85), channel_id=1, source_target_pairs={{0,32},{16,48},{32,0},{48,16},{64,96},{80,112},{96,64},{112,80},{1... | collective-permute-start | bytes 24584 | tf_op jit(solution)/shard_map/ppermute | solution.py:9
  182.6 11.7 %collective-permute-start.2 = (f32[128,16]{0,1:T(8,128)S(1)}, f32[128,16]{0,1:T(8,128)S(1)}, u32[]{:S(2)}, u32[]{:S(2)}) collective-permute-start(f32[128,16]{0,1:T(8,128)S(1)} %add.86), channel_id=1, source_target_pairs={{0,64},{16,80},{32,96},{48,112},{64,0},{80,16},{96,32},{112,48},{1... | collective-permute-start | bytes 24584 | tf_op jit(solution)/shard_map/ppermute | solution.py:9
  194.3 7.6 %collective-permute-start.3 = (f32[128,16]{0,1:T(8,128)S(1)}, f32[128,16]{0,1:T(8,128)S(1)}, u32[]{:S(2)}, u32[]{:S(2)}) collective-permute-start(f32[128,16]{0,1:T(8,128)S(1)} %add.87), channel_id=1, source_target_pairs={{0,128},{16,144},{32,160},{48,176},{64,192},{80,208},{96,224},{112... | collective-permute-start | bytes 24584 | tf_op jit(solution)/shard_map/ppermute | solution.py:9
  207.7 11.2 %all-to-all-start.5 = ((f32[16,128,16]{1,2,0:T(8,128)}), f32[16,128,16]{1,2,0:T(8,128)S(1)}, u32[]{:S(2)}, u32[]{:S(2)}) async-start(f32[16,128,16]{1,2,0:T(8,128)} %broadcast_in_dim.19), calls=%async_computation.6 | async-start | bytes 262144 | tf_op jit(solution)/shard_map/all_to_all | solution.py:15
Sparse Core Ops, SparseCore 0:
  9.9 63.7 all-gather.1
  96.8 71.8 reduce-scatter.1

commit v3 on v0

--- a/solution.py
+++ b/solution.py
@@ -160,8 +160,7 @@
     ).reshape(total, width)
     d_expert = jnp.sum(d_returned[slot_index].astype(jnp.float32), axis=1)
     pieces = [
-        row_major(contract_rows(slot_rows, d_pre_gate)),
-        row_major(contract_rows(slot_rows, d_pre_up)),
+        row_major(contract_rows(slot_rows, jnp.concatenate([d_pre_gate, d_pre_up], axis=1))),
         row_major(contract_rows(d_inbox, hidden_rows)),
     ]
     shares = lax.psum_scatter(

time: 227 us -> 227 us (level)
    dot_general x4 -> x3, matrix products: 5.72 us -> 5.51 us  [contract_rows(): lax.dot_general(left, right, (((0,), (0,)), ((), ())), preferred_element_...]
  transfers between devices with their start and end apart: 16 -> 16, of which waited for: 11 -> 11; matrix products, arithmetic and copies ran while one was open for 31% -> 30% of each run, Pallas kernels for 0% -> 0%
where the time goes in v3:
time: 227 us; the launch traced here: 226 us
  waiting for transfers between devices  72.2 us (32%)
  starting transfers between devices  50.1 us (22%)
  matrix products  34.8 us (15%)
  local copies, waits for them, and re-layouts  26.8 us (12%)
  other arithmetic  25.3 us (11%)
  between operations  17 us (7%)
    all_gather x1, waiting for transfers between devices, on_device(): gathered = lax.all_gather(held, 'dp', axis=1, tiled=True)  22.6 us
    all_to_all x1, waiting for transfers between devices, on_device(): lax.all_to_all(result, 'expert', split_axis=0, concat_axis=0, tiled=True)  15.2 us
    ppermute x8, waiting for transfers between devices, swapped(): lax.ppermute(array, axis, [(i, i ^ 1 << stride) for i in range(lax.axis_s...  13.3 us
    ppermute x8, starting transfers between devices, swapped(): lax.ppermute(array, axis, [(i, i ^ 1 << stride) for i in range(lax.axis_s...  10.9 us
    all_to_all x1, waiting for transfers between devices, on_device(): lax.all_to_all(outbox, 'expert', split_axis=0, concat_axis=0, tiled=True)  10 us
    all_to_all x1, starting transfers between devices, on_device(): lax.all_to_all(outbox, 'expert', split_axis=0, concat_axis=0, tiled=True)  7.61 us
    all_to_all x1, starting transfers between devices, on_device(): lax.all_to_all(result, 'expert', split_axis=0, concat_axis=0, tiled=True)  7.4 us
    all_to_all x1, starting transfers between devices, on_device(): lax.all_to_all(d_rows.reshape(groups, capacity, width), 'expert', split_a...  6.46 us
  transfers between devices with their start and end apart: 16, of which 11 were waited for; matrix products, arithmetic and copies ran while one was open for 30% of the time, Pallas kernels for 0%

profile of v3, /device:TPU:2, one launch (start us, length us, event | category | flops | bytes accessed | tf_op | source)
XLA Modules:
  0.0 226.2 jit_solution(6985422025171004675)
XLA Ops:
  12.1 3.4 %scatter_custom_fusion = bf16[384,2048]{1,0:T(8,128)(2,1)} fusion(s32[256]{0:T(256)S(1)} %bitcast.88, bf16[256,2048]{1,0:T(8,128)(2,1)S(1)} %reshape.199, bf16[]{:T(256)} %constant.16.clone.1), kind=kCustom, calls=%fused_computation.37 | custom fusion | bytes 1572866 | tf_op jit(solution)/shard_map/scatter | solution.py:57
  15.5 7.6 %all-to-all-start = ((bf16[16,24,2048]{2,1,0:T(8,128)(2,1)}), bf16[16,24,2048]{2,1,0:T(8,128)(2,1)S(1)}, u32[]{:S(2)}, u32[]{:S(2)}) async-start(bf16[16,24,2048]{2,1,0:T(8,128)(2,1)} %bitcast.3), calls=%async_computation | async-start | bytes 3145728 | tf_op jit(solution)/shard_map/all_to_all | solution.py:122
  23.1 2.5 %mul.155 = f32[128,2,2048]{2,1,0:T(2,128)} broadcast(bf16[128,2048]{1,0:T(8,128)(2,1)S(1)} %copy-done.3), dimensions={0,2} | broadcast | bytes 2621440 | tf_op jit(solution)/shard_map/mul | solution.py:142
  25.6 3.7 %mul.156 = f32[256,2048]{1,0:T(8,128)} reshape(f32[128,2,2048]{2,1,0:T(2,128)} %mul.155) | data formatting | bytes 4194304 | tf_op jit(solution)/shard_map/mul | solution.py:142
  29.8 4.7 %scatter_custom_fusion.1 = bf16[384,2048]{1,0:T(8,128)(2,1)} fusion(s32[256]{0:T(256)S(1)} %bitcast.89, f32[256,2048]{1,0:T(8,128)} %mul.156, f32[256]{0:T(256)S(1)} %div.42, bf16[]{:T(256)} %constant.16.clone.1), kind=kCustom, calls=%fused_computation.34 | custom fusion | flops 1048576 | bytes 3671042 | tf_op jit(solution)/shard_map/scatter | solution.py:57
  34.5 10.0 %all-to-all-done = bf16[16,24,2048]{2,1,0:T(8,128)(2,1)S(1)} async-done(((bf16[16,24,2048]{2,1,0:T(8,128)(2,1)}), bf16[16,24,2048]{2,1,0:T(8,128)(2,1)S(1)}, u32[]{:S(2)}, u32[]{:S(2)}) %all-to-all-start) | async-done | bytes 1572896 | tf_op jit(solution)/shard_map/all_to_all | solution.py:122
  44.5 6.3 %all-to-all-start.2 = ((bf16[16,24,2048]{2,1,0:T(8,128)(2,1)}), bf16[16,24,2048]{2,1,0:T(8,128)(2,1)S(1)}, u32[]{:S(2)}, u32[]{:S(2)}) async-start(bf16[16,24,2048]{2,1,0:T(8,128)(2,1)} %bitcast.84), calls=%async_computation.2 | async-start | bytes 3145728 | tf_op jit(solution)/shard_map/all_to_all | solution.py:144
  51.0 22.6 %all-gather.2.cloned.1.call-done = bf16[3,2048,768]{2,1,0:T(8,128)(2,1)} async-done(((bf16[3,128,768]{2,1,0:T(8,128)(2,1)}), bf16[3,2048,768]{2,1,0:T(8,128)(2,1)}) %all-gather.2.cloned.1.call-update) | async-done | bytes 9437200 | tf_op jit(solution)/shard_map/all_gather | solution.py:117
  73.6 4.3 %fusion.2 = f32[384,768]{1,0:T(8,128)} fusion(bf16[384,2048]{1,0:T(8,128)(2,1)S(1)} %bitcast.79, bf16[3,2048,768]{2,1,0:T(8,128)(2,1)} %all-gather.2.cloned.1.call-done), kind=kOutput, calls=%fused_computation.12 | convolution fusion | flops 1207959552 | bytes 5898240 | tf_op jit(solution)/shard_map/dot_general | solution.py:61
  77.9 4.3 %fusion.3 = f32[384,768]{1,0:T(8,128)} fusion(bf16[384,2048]{1,0:T(8,128)(2,1)S(1)} %bitcast.80, bf16[3,2048,768]{2,1,0:T(8,128)(2,1)} %all-gather.2.cloned.1.call-done), kind=kOutput, calls=%fused_computation.13 | convolution fusion | flops 1207959552 | bytes 5898240 | tf_op jit(solution)/shard_map/dot_general | solution.py:62
  82.2 4.2 %multiply_convert_fusion.1 = (bf16[384,768]{1,0:T(8,128)(2,1)S(1)}, bf16[384,768]{1,0:T(8,128)(2,1)S(1)}, bf16[384,768]{1,0:T(8,128)(2,1)S(1)}) fusion(f32[384,768]{1,0:T(8,128)} %fusion.2, f32[384,768]{1,0:T(8,128)} %fusion.3, bf16[384,2048]{1,0:T(8,128)(2,1)S(1)} %bitcast.82, bf16[3,2048,768]{2,1,0:T(8,128)(2,1)} %all-gather.2.cloned.1.call-done), kind=kOutput, calls=%fused_computation.25 | convolution fusion | flops 1212678144 | bytes 8847360 | tf_op jit(solution)/shard_map/dot_general | solution.py:71
  88.4 3.5 %fusion.6 = f32[2048,1536]{1,0:T(8,128)S(1)} fusion(bf16[384,2048]{1,0:T(8,128)(2,1)S(1)} %bitcast.81, bf16[384,768]{1,0:T(8,128)(2,1)S(1)} %get-tuple-element.24, bf16[384,768]{1,0:T(8,128)(2,1)S(1)} %get-tuple-element.25), kind=kOutput, calls=%fused_computation.21 | convolution fusion | flops 2418278400 | bytes 15335424 | tf_op jit(solution)/shard_map/dot_general | solution.py:88
  91.8 4.8 %fusion = bf16[2048,2304]{1,0:T(8,128)(2,1)} fusion(f32[2048,768]{1,0:T(8,128)S(1)} %fusion.27, f32[2048,1536]{1,0:T(8,128)S(1)} %fusion.6), kind=kLoop, calls=%fused_computation.5 | loop fusion | flops 14155776 | bytes 28311552 | tf_op jit(solution)/shard_map/convert_element_type | solution.py:167
  97.8 4.5 %convolution_convert_fusion = bf16[384,2048]{1,0:T(8,128)(2,1)} fusion(bf16[384,768]{1,0:T(8,128)(2,1)S(1)} %copy-done.10, bf16[3,2048,768]{2,1,0:T(8,128)(2,1)} %all-gather.2.cloned.1.call-done), kind=kOutput, calls=%fused_computation.10 | convolution fusion | flops 1208745984 | bytes 5308416 | tf_op jit(solution)/shard_map/dot_general | solution.py:64
  102.3 7.4 %all-to-all-start.1 = ((bf16[16,24,2048]{2,1,0:T(8,128)(2,1)}), bf16[16,24,2048]{2,1,0:T(8,128)(2,1)S(1)}, u32[]{:S(2)}, u32[]{:S(2)}) async-start(bf16[16,24,2048]{2,1,0:T(8,128)(2,1)} %bitcast.86), calls=%async_computation.1 | async-start | bytes 3145728 | tf_op jit(solution)/shard_map/all_to_all | solution.py:135
  111.3 5.1 %fusion.1 = f32[384,2048]{1,0:T(8,128)} fusion(bf16[384,768]{1,0:T(8,128)(2,1)S(1)} %copy-done.8, bf16[3,2048,768]{2,1,0:T(8,128)(2,1)} %all-gather.2.cloned.1.call-done), kind=kOutput, calls=%fused_computation.11 | convolution fusion | flops 1207959552 | bytes 6881280 | tf_op jit(solution)/shard_map/dot_general | solution.py:76
  116.3 15.2 %all-to-all-done.1 = bf16[16,24,2048]{2,1,0:T(8,128)(2,1)S(1)} async-done(((bf16[16,24,2048]{2,1,0:T(8,128)(2,1)}), bf16[16,24,2048]{2,1,0:T(8,128)(2,1)S(1)}, u32[]{:S(2)}, u32[]{:S(2)}) %all-to-all-start.1) | async-done | bytes 1572896 | tf_op jit(solution)/shard_map/all_to_all | solution.py:135
  131.5 2.4 %gather_fusion = bf16[256,2048]{1,0:T(8,128)(2,1)} fusion(bf16[384,2048]{1,0:T(8,128)(2,1)S(1)} %bitcast.78, s32[1024]{0:T(1024)S(1)} %pad_clamp_fusion), kind=kCustom, calls=%fused_computation | custom fusion | bytes 2098176 | tf_op jit(solution)/shard_map/gather | solution.py:138
  133.9 2.4 %reshape.213 = f32[128,2,2048]{2,1,0:T(2,128)S(1)} reshape(bf16[256,2048]{1,0:T(8,128)(2,1)} %gather_fusion) | data formatting | bytes 3145728 | tf_op jit(solution)/shard_map/convert_element_type | solution.py:138
  136.3 6.1 %multiply_reduce_fusion = (f32[128,2]{1,0:T(8,128)S(1)}, bf16[128,2048]{1,0:T(8,128)(2,1)}) fusion(f32[128,2,2048]{2,1,0:T(2,128)S(1)} %reshape.213, f32[128,2048]{1,0:T(8,128)} %convert_element_type.54, f32[128,2]{1,0:T(8,128)S(1)} %copy.38), kind=kLoop, calls=%fused_computation.18 | loop fusion | flops 1834752 | bytes 3672064 | tf_op jit(solution)/shard_map/reduce_sum | solution.py:141
  143.4 6.3 %all-to-all-start.4 = ((f32[16,128,16]{1,2,0:T(8,128)}), f32[16,128,16]{1,2,0:T(8,128)S(1)}, u32[]{:S(2)}, u32[]{:S(2)}) async-start(f32[16,128,16]{1,2,0:T(8,128)} %bitcast.76), calls=%async_computation.4 | async-start | bytes 262144 | tf_op jit(solution)/shard_map/all_to_all | solution.py:23
  149.7 5.6 %add_convert_fusion = bf16[384,2048]{1,0:T(8,128)(2,1)} fusion(f32[384,2048]{1,0:T(8,128)} %fusion.1, bf16[384,768]{1,0:T(8,128)(2,1)S(1)} %copy-done.6, bf16[3,2048,768]{2,1,0:T(8,128)(2,1)} %all-gather.2.cloned.1.call-done), kind=kOutput, calls=%fused_computation.9 | convolution fusion | flops 1209532416 | bytes 8454144 | tf_op jit(solution)/shard_map/dot_general | solution.py:77
  156.1 6.5 %all-to-all-start.3 = ((bf16[16,24,2048]{2,1,0:T(8,128)(2,1)}), bf16[16,24,2048]{2,1,0:T(8,128)(2,1)S(1)}, u32[]{:S(2)}, u32[]{:S(2)}) async-start(bf16[16,24,2048]{2,1,0:T(8,128)(2,1)} %bitcast.85), calls=%async_computation.3 | async-start | bytes 3145728 | tf_op jit(solution)/shard_map/all_to_all | solution.py:158
  162.6 6.2 %reduce-scatter.2.cloned.1.call-done = bf16[128,2304]{1,0:T(8,128)(2,1)} async-done(((bf16[2048,2304]{1,0:T(8,128)(2,1)}), bf16[128,2304]{1,0:T(8,128)(2,1)}) %reduce-scatter.2.cloned.1.call-update) | async-done | bytes 589840 | tf_op jit(solution)/shard_map/reduce_scatter | solution.py:166
  172.2 2.7 %collective-permute-start.5 = (bf16[3,128,768]{2,1,0:T(8,128)(2,1)}, bf16[3,128,768]{2,1,0:T(8,128)(2,1)}, u32[]{:S(2)}, u32[]{:S(2)}) collective-permute-start(bf16[3,128,768]{2,1,0:T(8,128)(2,1)} %pad_maximum_fusion.1), channel_id=1, source_target_pairs={{0,2},{1,3},{2,0},{3,1},{4,6},{5,7},{6,4},{7,5},{8,10},{9,11},{10,... | collective-permute-start | bytes 1769480 | tf_op jit(solution)/shard_map/ppermute | solution.py:9
  178.9 3.6 %collective-permute-done.1 = f32[128,16]{0,1:T(8,128)S(1)} collective-permute-done((f32[128,16]{0,1:T(8,128)S(1)}, f32[128,16]{0,1:T(8,128)S(1)}, u32[]{:S(2)}, u32[]{:S(2)}) %collective-permute-start.1) | collective-permute-done | bytes 8224 | tf_op jit(solution)/shard_map/ppermute | solution.py:9
  191.6 2.8 %reduce_sum.118 = f32[128,2048]{1,0:T(8,128)S(1)} reduce(f32[128,2,2048]{2,1,0:T(2,128)S(1)} %reshape.214, f32[]{:T(128)} %constant.15.clone.1), dimensions={1}, to_apply=%region_9.10 | reduce | flops 262144 | bytes 3145732 | tf_op jit(solution)/shard_map/reduce_sum | solution.py:161
  194.3 3.0 %collective-permute-start.3 = (f32[128,16]{0,1:T(8,128)S(1)}, f32[128,16]{0,1:T(8,128)S(1)}, u32[]{:S(2)}, u32[]{:S(2)}) collective-permute-start(f32[128,16]{0,1:T(8,128)S(1)} %add.87), channel_id=1, source_target_pairs={{0,128},{16,144},{32,160},{48,176},{64,192},{80,208},{96,224},{112... | collective-permute-start | bytes 24584 | tf_op jit(solution)/shard_map/ppermute | solution.py:9
  198.4 3.6 %collective-permute-done.3 = f32[128,16]{0,1:T(8,128)S(1)} collective-permute-done((f32[128,16]{0,1:T(8,128)S(1)}, f32[128,16]{0,1:T(8,128)S(1)}, u32[]{:S(2)}, u32[]{:S(2)}) %collective-permute-start.3) | collective-permute-done | bytes 8224 | tf_op jit(solution)/shard_map/ppermute | solution.py:9
  202.0 4.2 %collective-permute-done.5 = bf16[3,128,768]{2,1,0:T(8,128)(2,1)} collective-permute-done((bf16[3,128,768]{2,1,0:T(8,128)(2,1)}, bf16[3,128,768]{2,1,0:T(8,128)(2,1)}, u32[]{:S(2)}, u32[]{:S(2)}) %collective-permute-start.5) | collective-permute-done | bytes 589856 | tf_op jit(solution)/shard_map/ppermute | solution.py:9
  207.5 4.8 %all-to-all-start.5 = ((f32[16,128,16]{1,2,0:T(8,128)}), f32[16,128,16]{1,2,0:T(8,128)S(1)}, u32[]{:S(2)}, u32[]{:S(2)}) async-start(f32[16,128,16]{1,2,0:T(8,128)} %broadcast_in_dim.19), calls=%async_computation.6 | async-start | bytes 262144 | tf_op jit(solution)/shard_map/all_to_all | solution.py:15
  214.6 4.2 %all-to-all-done.5 = f32[16,128,16]{1,2,0:T(8,128)S(1)} async-done(((f32[16,128,16]{1,2,0:T(8,128)}), f32[16,128,16]{1,2,0:T(8,128)S(1)}, u32[]{:S(2)}, u32[]{:S(2)}) %all-to-all-start.5) | async-done | bytes 131104 | tf_op jit(solution)/shard_map/all_to_all | solution.py:15
  (98 shorter events, 31.0 us)
Async XLA Ops:
  7.2 22.1 %copy-start = (bf16[2048,16]{0,1:T(8,128)(2,1)S(1)}, bf16[2048,16]{0,1:T(8,128)(2,1)}, u32[]{:S(2)}) copy-start(bf16[2048,16]{0,1:T(8,128)(2,1)} %param.12) | copy-start | bytes 196612
  7.2 2.2 copy-start.11
  7.2 3.7 %copy-start.1 = (bf16[128,2048]{1,0:T(8,128)(2,1)S(1)}, bf16[128,2048]{1,0:T(8,128)(2,1)}, u32[]{:S(2)}) copy-start(bf16[128,2048]{1,0:T(8,128)(2,1)} %param.8) | copy-start | bytes 1572868
  7.2 66.4 %all-gather.2.cloned.1.call-start = ((), (), s32[]{:S(2)}) async-start(), calls=%async_computation.7 | async-start | bytes 10027008 | tf_op jit(solution)/shard_map/all_gather | solution.py:117
  15.5 7.6 %copy-start.3 = (bf16[128,2048]{1,0:T(8,128)(2,1)S(1)}, bf16[128,2048]{1,0:T(8,128)(2,1)}, u32[]{:S(2)}) copy-start(bf16[128,2048]{1,0:T(8,128)(2,1)} %param.9) | copy-start | bytes 1572868
  15.5 29.0 %all-to-all-start = ((bf16[16,24,2048]{2,1,0:T(8,128)(2,1)}), bf16[16,24,2048]{2,1,0:T(8,128)(2,1)S(1)}, u32[]{:S(2)}, u32[]{:S(2)}) async-start(bf16[16,24,2048]{2,1,0:T(8,128)(2,1)} %bitcast.3), calls=%async_computation | async-start | bytes 3145728 | tf_op jit(solution)/shard_map/all_to_all | solution.py:122
  44.5 37.7 %all-to-all-start.2 = ((bf16[16,24,2048]{2,1,0:T(8,128)(2,1)}), bf16[16,24,2048]{2,1,0:T(8,128)(2,1)S(1)}, u32[]{:S(2)}, u32[]{:S(2)}) async-start(bf16[16,24,2048]{2,1,0:T(8,128)(2,1)} %bitcast.84), calls=%async_computation.2 | async-start | bytes 3145728 | tf_op jit(solution)/shard_map/all_to_all | solution.py:144
  50.8 117.9 %reduce-scatter.2.cloned.1.call-start = ((), (), s32[]{:S(2)}) async-start(), calls=%async_computation.8 | async-start | bytes 10027008 | tf_op jit(solution)/shard_map/reduce_scatter | solution.py:166
  86.4 1.9 copy-start.9
  86.5 1.9 copy-start.5
  86.5 1.9 copy-start.7
  96.7 1.1 copy-start.10
  102.3 7.6 %copy-start.4 = (bf16[128,2048]{1,0:T(8,128)(2,1)S(1)}, bf16[128,2048]{1,0:T(8,128)(2,1)}, u32[]{:S(2)}) copy-start(bf16[128,2048]{1,0:T(8,128)(2,1)} %param.9) | copy-start | bytes 1572868
  102.3 29.3 %all-to-all-start.1 = ((bf16[16,24,2048]{2,1,0:T(8,128)(2,1)}), bf16[16,24,2048]{2,1,0:T(8,128)(2,1)S(1)}, u32[]{:S(2)}, u32[]{:S(2)}) async-start(bf16[16,24,2048]{2,1,0:T(8,128)(2,1)} %bitcast.86), calls=%async_computation.1 | async-start | bytes 3145728 | tf_op jit(solution)/shard_map/all_to_all | solution.py:135
  109.7 1.6 copy-start.8
  136.3 6.2 %copy-start.2 = (bf16[128,2048]{1,0:T(8,128)(2,1)S(1)}, bf16[128,2048]{1,0:T(8,128)(2,1)}, u32[]{:S(2)}) copy-start(bf16[128,2048]{1,0:T(8,128)(2,1)} %param.8) | copy-start | bytes 1572868
  136.3 13.4 %copy-start.6 = (bf16[384,768]{1,0:T(8,128)(2,1)S(1)}, bf16[384,768]{1,0:T(8,128)(2,1)}, u32[]{:S(2)}) copy-start(bf16[384,768]{1,0:T(8,128)(2,1)} %copy-done.5) | copy-start | bytes 1769476
  143.4 12.7 %all-to-all-start.4 = ((f32[16,128,16]{1,2,0:T(8,128)}), f32[16,128,16]{1,2,0:T(8,128)S(1)}, u32[]{:S(2)}, u32[]{:S(2)}) async-start(f32[16,128,16]{1,2,0:T(8,128)} %bitcast.76), calls=%async_computation.4 | async-start | bytes 262144 | tf_op jit(solution)/shard_map/all_to_all | solution.py:23
  156.1 30.7 %all-to-all-start.3 = ((bf16[16,24,2048]{2,1,0:T(8,128)(2,1)}), bf16[16,24,2048]{2,1,0:T(8,128)(2,1)S(1)}, u32[]{:S(2)}, u32[]{:S(2)}) async-start(bf16[16,24,2048]{2,1,0:T(8,128)(2,1)} %bitcast.85), calls=%async_computation.3 | async-start | bytes 3145728 | tf_op jit(solution)/shard_map/all_to_all | solution.py:158
  162.5 21.1 %copy-start.12 = (s32[16]{0:T(128)S(1)}, s32[16]{0:T(128)}, u32[]{:S(2)}) copy-start(s32[16]{0:T(128)} %param.11) | copy-start | bytes 196
  170.8 31.2 %collective-permute-start.4 = (bf16[3,128,768]{2,1,0:T(8,128)(2,1)}, bf16[3,128,768]{2,1,0:T(8,128)(2,1)}, u32[]{:S(2)}, u32[]{:S(2)}) collective-permute-start(bf16[3,128,768]{2,1,0:T(8,128)(2,1)} %pad_maximum_fusion.1), channel_id=1, source_target_pairs={{0,1},{1,0},{2,3},{3,2},{4,5},{5,4},{6,7},{7,6},{8,9},{9,8},{10,11... | collective-permute-start | bytes 1769480 | tf_op jit(solution)/shard_map/ppermute | solution.py:9
  172.2 34.0 %collective-permute-start.5 = (bf16[3,128,768]{2,1,0:T(8,128)(2,1)}, bf16[3,128,768]{2,1,0:T(8,128)(2,1)}, u32[]{:S(2)}, u32[]{:S(2)}) collective-permute-start(bf16[3,128,768]{2,1,0:T(8,128)(2,1)} %pad_maximum_fusion.1), channel_id=1, source_target_pairs={{0,2},{1,3},{2,0},{3,1},{4,6},{5,7},{6,4},{7,5},{8,10},{9,11},{10,... | collective-permute-start | bytes 1769480 | tf_op jit(solution)/shard_map/ppermute | solution.py:9
  174.9 31.3 %collective-permute-start.6 = (bf16[3,128,768]{2,1,0:T(8,128)(2,1)}, bf16[3,128,768]{2,1,0:T(8,128)(2,1)}, u32[]{:S(2)}, u32[]{:S(2)}) collective-permute-start(bf16[3,128,768]{2,1,0:T(8,128)(2,1)} %pad_maximum_fusion.1), channel_id=1, source_target_pairs={{0,4},{1,5},{2,6},{3,7},{4,0},{5,1},{6,2},{7,3},{8,12},{9,13},{10,... | collective-permute-start | bytes 1769480 | tf_op jit(solution)/shard_map/ppermute | solution.py:9
  175.8 31.1 %collective-permute-start.7 = (bf16[3,128,768]{2,1,0:T(8,128)(2,1)}, bf16[3,128,768]{2,1,0:T(8,128)(2,1)}, u32[]{:S(2)}, u32[]{:S(2)}) collective-permute-start(bf16[3,128,768]{2,1,0:T(8,128)(2,1)} %pad_maximum_fusion.1), channel_id=1, source_target_pairs={{0,8},{1,9},{2,10},{3,11},{4,12},{5,13},{6,14},{7,15},{8,0},{9,1},... | collective-permute-start | bytes 1769480 | tf_op jit(solution)/shard_map/ppermute | solution.py:9
  177.8 1.2 collective-permute-start
  178.9 3.7 %collective-permute-start.1 = (f32[128,16]{0,1:T(8,128)S(1)}, f32[128,16]{0,1:T(8,128)S(1)}, u32[]{:S(2)}, u32[]{:S(2)}) collective-permute-start(f32[128,16]{0,1:T(8,128)S(1)} %add.85), channel_id=1, source_target_pairs={{0,32},{16,48},{32,0},{48,16},{64,96},{80,112},{96,64},{112,80},{1... | collective-permute-start | bytes 24584 | tf_op jit(solution)/shard_map/ppermute | solution.py:9
  182.6 11.7 %collective-permute-start.2 = (f32[128,16]{0,1:T(8,128)S(1)}, f32[128,16]{0,1:T(8,128)S(1)}, u32[]{:S(2)}, u32[]{:S(2)}) collective-permute-start(f32[128,16]{0,1:T(8,128)S(1)} %add.86), channel_id=1, source_target_pairs={{0,64},{16,80},{32,96},{48,112},{64,0},{80,16},{96,32},{112,48},{1... | collective-permute-start | bytes 24584 | tf_op jit(solution)/shard_map/ppermute | solution.py:9
  194.3 7.6 %collective-permute-start.3 = (f32[128,16]{0,1:T(8,128)S(1)}, f32[128,16]{0,1:T(8,128)S(1)}, u32[]{:S(2)}, u32[]{:S(2)}) collective-permute-start(f32[128,16]{0,1:T(8,128)S(1)} %add.87), channel_id=1, source_target_pairs={{0,128},{16,144},{32,160},{48,176},{64,192},{80,208},{96,224},{112... | collective-permute-start | bytes 24584 | tf_op jit(solution)/shard_map/ppermute | solution.py:9
  207.5 11.2 %all-to-all-start.5 = ((f32[16,128,16]{1,2,0:T(8,128)}), f32[16,128,16]{1,2,0:T(8,128)S(1)}, u32[]{:S(2)}, u32[]{:S(2)}) async-start(f32[16,128,16]{1,2,0:T(8,128)} %broadcast_in_dim.19), calls=%async_computation.6 | async-start | bytes 262144 | tf_op jit(solution)/shard_map/all_to_all | solution.py:15
Sparse Core Ops, SparseCore 0:
  9.9 63.7 all-gather.1
  96.8 71.8 reduce-scatter.1

commit v4 on v3

--- a/solution.py
+++ b/solution.py
@@ -25,12 +25,12 @@
     )
     piece = jnp.sum(parts, axis=0)
     piece, companion = lax.optimization_barrier((piece, companion))
-    arrivals = [swapped(companion, "expert", bit_level) for bit_level in range(groups.bit_length() - 1)]
+    arrivals = [swapped(companion, "expert", bit_level) for bit_level in range(groups.bit_length() - 1)][::-1]
     for bit_level in range(replicas.bit_length() - 1):
         piece = piece + swapped(piece, "dp", bit_level)
     piece, arrivals = lax.optimization_barrier((piece, arrivals))
     chosen = companion
-    for bit_level, arrived in enumerate(arrivals):
+    for bit_level, arrived in zip(range(len(arrivals) - 1, -1, -1), arrivals):
         chosen = jnp.where(partner == jnp.bitwise_xor(my_index, 1 << bit_level), arrived, chosen)
     return gather_by_exchange(piece, "expert"), chosen
 

time: 227 us -> 229 us (level)
  starting transfers between devices: 50.1 us -> 52.7 us
    all_to_all x1, starting transfers between devices: 4.81 us -> 7.45 us  [gather_by_exchange(): joined = lax.all_to_all(copies, axis, 0, 0, tiled=True)]
where the time goes in v4:
time: 229 us; the launch traced here: 227 us
  waiting for transfers between devices  70.5 us (31%)
  starting transfers between devices  52.7 us (23%)
  matrix products  34.8 us (15%)
  local copies, waits for them, and re-layouts  26.8 us (12%)
  other arithmetic  25.3 us (11%)
  between operations  17 us (7%)
    all_gather x1, waiting for transfers between devices, on_device(): gathered = lax.all_gather(held, 'dp', axis=1, tiled=True)  22.6 us
    all_to_all x1, waiting for transfers between devices, on_device(): lax.all_to_all(result, 'expert', split_axis=0, concat_axis=0, tiled=True)  15.2 us
    ppermute x8, waiting for transfers between devices, swapped(): lax.ppermute(array, axis, [(i, i ^ 1 << stride) for i in range(lax.axis_s...  11.5 us
    ppermute x8, starting transfers between devices, swapped(): lax.ppermute(array, axis, [(i, i ^ 1 << stride) for i in range(lax.axis_s...  10.9 us
    all_to_all x1, waiting for transfers between devices, on_device(): lax.all_to_all(outbox, 'expert', split_axis=0, concat_axis=0, tiled=True)  10 us
    all_to_all x1, starting transfers between devices, on_device(): lax.all_to_all(outbox, 'expert', split_axis=0, concat_axis=0, tiled=True)  7.61 us
    all_to_all x1, starting transfers between devices, gather_by_exchange(): joined = lax.all_to_all(copies, axis, 0, 0, tiled=True)  7.45 us
    all_to_all x1, starting transfers between devices, on_device(): lax.all_to_all(result, 'expert', split_axis=0, concat_axis=0, tiled=True)  7.4 us
  transfers between devices with their start and end apart: 16, of which 11 were waited for; matrix products, arithmetic and copies ran while one was open for 30% of the time, Pallas kernels for 0%

profile of v4, /device:TPU:2, one launch (start us, length us, event | category | flops | bytes accessed | tf_op | source)
XLA Modules:
  0.0 227.2 jit_solution(69392518844005767)
XLA Ops:
  12.1 3.4 %scatter_custom_fusion = bf16[384,2048]{1,0:T(8,128)(2,1)} fusion(s32[256]{0:T(256)S(1)} %bitcast.88, bf16[256,2048]{1,0:T(8,128)(2,1)S(1)} %reshape.199, bf16[]{:T(256)} %constant.16.clone.1), kind=kCustom, calls=%fused_computation.37 | custom fusion | bytes 1572866 | tf_op jit(solution)/shard_map/scatter | solution.py:57
  15.5 7.6 %all-to-all-start = ((bf16[16,24,2048]{2,1,0:T(8,128)(2,1)}), bf16[16,24,2048]{2,1,0:T(8,128)(2,1)S(1)}, u32[]{:S(2)}, u32[]{:S(2)}) async-start(bf16[16,24,2048]{2,1,0:T(8,128)(2,1)} %bitcast.3), calls=%async_computation | async-start | bytes 3145728 | tf_op jit(solution)/shard_map/all_to_all | solution.py:122
  23.1 2.5 %mul.155 = f32[128,2,2048]{2,1,0:T(2,128)} broadcast(bf16[128,2048]{1,0:T(8,128)(2,1)S(1)} %copy-done.3), dimensions={0,2} | broadcast | bytes 2621440 | tf_op jit(solution)/shard_map/mul | solution.py:142
  25.6 3.7 %mul.156 = f32[256,2048]{1,0:T(8,128)} reshape(f32[128,2,2048]{2,1,0:T(2,128)} %mul.155) | data formatting | bytes 4194304 | tf_op jit(solution)/shard_map/mul | solution.py:142
  29.8 4.7 %scatter_custom_fusion.1 = bf16[384,2048]{1,0:T(8,128)(2,1)} fusion(s32[256]{0:T(256)S(1)} %bitcast.89, f32[256,2048]{1,0:T(8,128)} %mul.156, f32[256]{0:T(256)S(1)} %div.42, bf16[]{:T(256)} %constant.16.clone.1), kind=kCustom, calls=%fused_computation.34 | custom fusion | flops 1048576 | bytes 3671042 | tf_op jit(solution)/shard_map/scatter | solution.py:57
  34.5 10.0 %all-to-all-done = bf16[16,24,2048]{2,1,0:T(8,128)(2,1)S(1)} async-done(((bf16[16,24,2048]{2,1,0:T(8,128)(2,1)}), bf16[16,24,2048]{2,1,0:T(8,128)(2,1)S(1)}, u32[]{:S(2)}, u32[]{:S(2)}) %all-to-all-start) | async-done | bytes 1572896 | tf_op jit(solution)/shard_map/all_to_all | solution.py:122
  44.5 6.3 %all-to-all-start.2 = ((bf16[16,24,2048]{2,1,0:T(8,128)(2,1)}), bf16[16,24,2048]{2,1,0:T(8,128)(2,1)S(1)}, u32[]{:S(2)}, u32[]{:S(2)}) async-start(bf16[16,24,2048]{2,1,0:T(8,128)(2,1)} %bitcast.84), calls=%async_computation.2 | async-start | bytes 3145728 | tf_op jit(solution)/shard_map/all_to_all | solution.py:144
  51.0 22.6 %all-gather.2.cloned.1.call-done = bf16[3,2048,768]{2,1,0:T(8,128)(2,1)} async-done(((bf16[3,128,768]{2,1,0:T(8,128)(2,1)}), bf16[3,2048,768]{2,1,0:T(8,128)(2,1)}) %all-gather.2.cloned.1.call-update) | async-done | bytes 9437200 | tf_op jit(solution)/shard_map/all_gather | solution.py:117
  73.6 4.3 %fusion.2 = f32[384,768]{1,0:T(8,128)} fusion(bf16[384,2048]{1,0:T(8,128)(2,1)S(1)} %bitcast.79, bf16[3,2048,768]{2,1,0:T(8,128)(2,1)} %all-gather.2.cloned.1.call-done), kind=kOutput, calls=%fused_computation.12 | convolution fusion | flops 1207959552 | bytes 5898240 | tf_op jit(solution)/shard_map/dot_general | solution.py:61
  77.9 4.3 %fusion.3 = f32[384,768]{1,0:T(8,128)} fusion(bf16[384,2048]{1,0:T(8,128)(2,1)S(1)} %bitcast.80, bf16[3,2048,768]{2,1,0:T(8,128)(2,1)} %all-gather.2.cloned.1.call-done), kind=kOutput, calls=%fused_computation.13 | convolution fusion | flops 1207959552 | bytes 5898240 | tf_op jit(solution)/shard_map/dot_general | solution.py:62
  82.2 4.2 %multiply_convert_fusion.1 = (bf16[384,768]{1,0:T(8,128)(2,1)S(1)}, bf16[384,768]{1,0:T(8,128)(2,1)S(1)}, bf16[384,768]{1,0:T(8,128)(2,1)S(1)}) fusion(f32[384,768]{1,0:T(8,128)} %fusion.2, f32[384,768]{1,0:T(8,128)} %fusion.3, bf16[384,2048]{1,0:T(8,128)(2,1)S(1)} %bitcast.82, bf16[3,2048,768]{2,1,0:T(8,128)(2,1)} %all-gather.2.cloned.1.call-done), kind=kOutput, calls=%fused_computation.25 | convolution fusion | flops 1212678144 | bytes 8847360 | tf_op jit(solution)/shard_map/dot_general | solution.py:71
  88.4 3.5 %fusion.6 = f32[2048,1536]{1,0:T(8,128)S(1)} fusion(bf16[384,2048]{1,0:T(8,128)(2,1)S(1)} %bitcast.81, bf16[384,768]{1,0:T(8,128)(2,1)S(1)} %get-tuple-element.24, bf16[384,768]{1,0:T(8,128)(2,1)S(1)} %get-tuple-element.25), kind=kOutput, calls=%fused_computation.21 | convolution fusion | flops 2418278400 | bytes 15335424 | tf_op jit(solution)/shard_map/dot_general | solution.py:88
  91.8 4.8 %fusion = bf16[2048,2304]{1,0:T(8,128)(2,1)} fusion(f32[2048,768]{1,0:T(8,128)S(1)} %fusion.27, f32[2048,1536]{1,0:T(8,128)S(1)} %fusion.6), kind=kLoop, calls=%fused_computation.5 | loop fusion | flops 14155776 | bytes 28311552 | tf_op jit(solution)/shard_map/convert_element_type | solution.py:167
  97.8 4.5 %convolution_convert_fusion = bf16[384,2048]{1,0:T(8,128)(2,1)} fusion(bf16[384,768]{1,0:T(8,128)(2,1)S(1)} %copy-done.10, bf16[3,2048,768]{2,1,0:T(8,128)(2,1)} %all-gather.2.cloned.1.call-done), kind=kOutput, calls=%fused_computation.10 | convolution fusion | flops 1208745984 | bytes 5308416 | tf_op jit(solution)/shard_map/dot_general | solution.py:64
  102.3 7.4 %all-to-all-start.1 = ((bf16[16,24,2048]{2,1,0:T(8,128)(2,1)}), bf16[16,24,2048]{2,1,0:T(8,128)(2,1)S(1)}, u32[]{:S(2)}, u32[]{:S(2)}) async-start(bf16[16,24,2048]{2,1,0:T(8,128)(2,1)} %bitcast.86), calls=%async_computation.1 | async-start | bytes 3145728 | tf_op jit(solution)/shard_map/all_to_all | solution.py:135
  111.3 5.1 %fusion.1 = f32[384,2048]{1,0:T(8,128)} fusion(bf16[384,768]{1,0:T(8,128)(2,1)S(1)} %copy-done.8, bf16[3,2048,768]{2,1,0:T(8,128)(2,1)} %all-gather.2.cloned.1.call-done), kind=kOutput, calls=%fused_computation.11 | convolution fusion | flops 1207959552 | bytes 6881280 | tf_op jit(solution)/shard_map/dot_general | solution.py:76
  116.3 15.2 %all-to-all-done.1 = bf16[16,24,2048]{2,1,0:T(8,128)(2,1)S(1)} async-done(((bf16[16,24,2048]{2,1,0:T(8,128)(2,1)}), bf16[16,24,2048]{2,1,0:T(8,128)(2,1)S(1)}, u32[]{:S(2)}, u32[]{:S(2)}) %all-to-all-start.1) | async-done | bytes 1572896 | tf_op jit(solution)/shard_map/all_to_all | solution.py:135
  131.5 2.4 %gather_fusion = bf16[256,2048]{1,0:T(8,128)(2,1)} fusion(bf16[384,2048]{1,0:T(8,128)(2,1)S(1)} %bitcast.78, s32[1024]{0:T(1024)S(1)} %pad_clamp_fusion), kind=kCustom, calls=%fused_computation | custom fusion | bytes 2098176 | tf_op jit(solution)/shard_map/gather | solution.py:138
  133.9 2.4 %reshape.213 = f32[128,2,2048]{2,1,0:T(2,128)S(1)} reshape(bf16[256,2048]{1,0:T(8,128)(2,1)} %gather_fusion) | data formatting | bytes 3145728 | tf_op jit(solution)/shard_map/convert_element_type | solution.py:138
  136.3 6.1 %multiply_reduce_fusion = (f32[128,2]{1,0:T(8,128)S(1)}, bf16[128,2048]{1,0:T(8,128)(2,1)}) fusion(f32[128,2,2048]{2,1,0:T(2,128)S(1)} %reshape.213, f32[128,2048]{1,0:T(8,128)} %convert_element_type.54, f32[128,2]{1,0:T(8,128)S(1)} %copy.38), kind=kLoop, calls=%fused_computation.18 | loop fusion | flops 1834752 | bytes 3672064 | tf_op jit(solution)/shard_map/reduce_sum | solution.py:141
  143.4 6.3 %all-to-all-start.4 = ((f32[16,128,16]{1,2,0:T(8,128)}), f32[16,128,16]{1,2,0:T(8,128)S(1)}, u32[]{:S(2)}, u32[]{:S(2)}) async-start(f32[16,128,16]{1,2,0:T(8,128)} %bitcast.76), calls=%async_computation.4 | async-start | bytes 262144 | tf_op jit(solution)/shard_map/all_to_all | solution.py:23
  149.7 5.6 %add_convert_fusion = bf16[384,2048]{1,0:T(8,128)(2,1)} fusion(f32[384,2048]{1,0:T(8,128)} %fusion.1, bf16[384,768]{1,0:T(8,128)(2,1)S(1)} %copy-done.6, bf16[3,2048,768]{2,1,0:T(8,128)(2,1)} %all-gather.2.cloned.1.call-done), kind=kOutput, calls=%fused_computation.9 | convolution fusion | flops 1209532416 | bytes 8454144 | tf_op jit(solution)/shard_map/dot_general | solution.py:77
  156.1 6.5 %all-to-all-start.3 = ((bf16[16,24,2048]{2,1,0:T(8,128)(2,1)}), bf16[16,24,2048]{2,1,0:T(8,128)(2,1)S(1)}, u32[]{:S(2)}, u32[]{:S(2)}) async-start(bf16[16,24,2048]{2,1,0:T(8,128)(2,1)} %bitcast.85), calls=%async_computation.3 | async-start | bytes 3145728 | tf_op jit(solution)/shard_map/all_to_all | solution.py:158
  162.6 6.2 %reduce-scatter.2.cloned.1.call-done = bf16[128,2304]{1,0:T(8,128)(2,1)} async-done(((bf16[2048,2304]{1,0:T(8,128)(2,1)}), bf16[128,2304]{1,0:T(8,128)(2,1)}) %reduce-scatter.2.cloned.1.call-update) | async-done | bytes 589840 | tf_op jit(solution)/shard_map/reduce_scatter | solution.py:166
  174.3 2.8 %collective-permute-start.6 = (bf16[3,128,768]{2,1,0:T(8,128)(2,1)}, bf16[3,128,768]{2,1,0:T(8,128)(2,1)}, u32[]{:S(2)}, u32[]{:S(2)}) collective-permute-start(bf16[3,128,768]{2,1,0:T(8,128)(2,1)} %pad_maximum_fusion.1), channel_id=1, source_target_pairs={{0,2},{1,3},{2,0},{3,1},{4,6},{5,7},{6,4},{7,5},{8,10},{9,11},{10,... | collective-permute-start | bytes 1769480 | tf_op jit(solution)/shard_map/ppermute | solution.py:9
  178.9 3.6 %collective-permute-done.1 = f32[128,16]{0,1:T(8,128)S(1)} collective-permute-done((f32[128,16]{0,1:T(8,128)S(1)}, f32[128,16]{0,1:T(8,128)S(1)}, u32[]{:S(2)}, u32[]{:S(2)}) %collective-permute-start.1) | collective-permute-done | bytes 8224 | tf_op jit(solution)/shard_map/ppermute | solution.py:9
  189.2 2.4 %reshape.214 = f32[128,2,2048]{2,1,0:T(2,128)S(1)} reshape(bf16[256,2048]{1,0:T(8,128)(2,1)} %gather_fusion.1) | data formatting | bytes 3145728 | tf_op jit(solution)/shard_map/convert_element_type | solution.py:161
  191.6 2.8 %reduce_sum.118 = f32[128,2048]{1,0:T(8,128)S(1)} reduce(f32[128,2,2048]{2,1,0:T(2,128)S(1)} %reshape.214, f32[]{:T(128)} %constant.15.clone.1), dimensions={1}, to_apply=%region_9.10 | reduce | flops 262144 | bytes 3145732 | tf_op jit(solution)/shard_map/reduce_sum | solution.py:161
  194.3 3.0 %collective-permute-start.3 = (f32[128,16]{0,1:T(8,128)S(1)}, f32[128,16]{0,1:T(8,128)S(1)}, u32[]{:S(2)}, u32[]{:S(2)}) collective-permute-start(f32[128,16]{0,1:T(8,128)S(1)} %add.87), channel_id=1, source_target_pairs={{0,128},{16,144},{32,160},{48,176},{64,192},{80,208},{96,224},{112... | collective-permute-start | bytes 24584 | tf_op jit(solution)/shard_map/ppermute | solution.py:9
  198.4 3.6 %collective-permute-done.3 = f32[128,16]{0,1:T(8,128)S(1)} collective-permute-done((f32[128,16]{0,1:T(8,128)S(1)}, f32[128,16]{0,1:T(8,128)S(1)}, u32[]{:S(2)}, u32[]{:S(2)}) %collective-permute-start.3) | collective-permute-done | bytes 8224 | tf_op jit(solution)/shard_map/ppermute | solution.py:9
  205.8 7.5 %all-to-all-start.5 = ((f32[16,128,16]{1,2,0:T(8,128)}), f32[16,128,16]{1,2,0:T(8,128)S(1)}, u32[]{:S(2)}, u32[]{:S(2)}) async-start(f32[16,128,16]{1,2,0:T(8,128)} %broadcast_in_dim.19), calls=%async_computation.6 | async-start | bytes 262144 | tf_op jit(solution)/shard_map/all_to_all | solution.py:15
  215.5 4.2 %all-to-all-done.5 = f32[16,128,16]{1,2,0:T(8,128)S(1)} async-done(((f32[16,128,16]{1,2,0:T(8,128)}), f32[16,128,16]{1,2,0:T(8,128)S(1)}, u32[]{:S(2)}, u32[]{:S(2)}) %all-to-all-start.5) | async-done | bytes 131104 | tf_op jit(solution)/shard_map/all_to_all | solution.py:15
  (98 shorter events, 31.0 us)
Async XLA Ops:
  7.2 22.1 %copy-start = (bf16[2048,16]{0,1:T(8,128)(2,1)S(1)}, bf16[2048,16]{0,1:T(8,128)(2,1)}, u32[]{:S(2)}) copy-start(bf16[2048,16]{0,1:T(8,128)(2,1)} %param.12) | copy-start | bytes 196612
  7.2 2.2 copy-start.11
  7.2 3.7 %copy-start.1 = (bf16[128,2048]{1,0:T(8,128)(2,1)S(1)}, bf16[128,2048]{1,0:T(8,128)(2,1)}, u32[]{:S(2)}) copy-start(bf16[128,2048]{1,0:T(8,128)(2,1)} %param.8) | copy-start | bytes 1572868
  7.2 66.4 %all-gather.2.cloned.1.call-start = ((), (), s32[]{:S(2)}) async-start(), calls=%async_computation.7 | async-start | bytes 10027008 | tf_op jit(solution)/shard_map/all_gather | solution.py:117
  15.5 7.6 %copy-start.3 = (bf16[128,2048]{1,0:T(8,128)(2,1)S(1)}, bf16[128,2048]{1,0:T(8,128)(2,1)}, u32[]{:S(2)}) copy-start(bf16[128,2048]{1,0:T(8,128)(2,1)} %param.9) | copy-start | bytes 1572868
  15.5 29.0 %all-to-all-start = ((bf16[16,24,2048]{2,1,0:T(8,128)(2,1)}), bf16[16,24,2048]{2,1,0:T(8,128)(2,1)S(1)}, u32[]{:S(2)}, u32[]{:S(2)}) async-start(bf16[16,24,2048]{2,1,0:T(8,128)(2,1)} %bitcast.3), calls=%async_computation | async-start | bytes 3145728 | tf_op jit(solution)/shard_map/all_to_all | solution.py:122
  44.5 37.7 %all-to-all-start.2 = ((bf16[16,24,2048]{2,1,0:T(8,128)(2,1)}), bf16[16,24,2048]{2,1,0:T(8,128)(2,1)S(1)}, u32[]{:S(2)}, u32[]{:S(2)}) async-start(bf16[16,24,2048]{2,1,0:T(8,128)(2,1)} %bitcast.84), calls=%async_computation.2 | async-start | bytes 3145728 | tf_op jit(solution)/shard_map/all_to_all | solution.py:144
  50.8 117.9 %reduce-scatter.2.cloned.1.call-start = ((), (), s32[]{:S(2)}) async-start(), calls=%async_computation.8 | async-start | bytes 10027008 | tf_op jit(solution)/shard_map/reduce_scatter | solution.py:166
  86.4 1.9 copy-start.9
  86.5 1.9 copy-start.5
  86.5 1.9 copy-start.7
  96.7 1.1 copy-start.10
  102.3 7.6 %copy-start.4 = (bf16[128,2048]{1,0:T(8,128)(2,1)S(1)}, bf16[128,2048]{1,0:T(8,128)(2,1)}, u32[]{:S(2)}) copy-start(bf16[128,2048]{1,0:T(8,128)(2,1)} %param.9) | copy-start | bytes 1572868
  102.3 29.3 %all-to-all-start.1 = ((bf16[16,24,2048]{2,1,0:T(8,128)(2,1)}), bf16[16,24,2048]{2,1,0:T(8,128)(2,1)S(1)}, u32[]{:S(2)}, u32[]{:S(2)}) async-start(bf16[16,24,2048]{2,1,0:T(8,128)(2,1)} %bitcast.86), calls=%async_computation.1 | async-start | bytes 3145728 | tf_op jit(solution)/shard_map/all_to_all | solution.py:135
  109.7 1.6 copy-start.8
  136.3 6.2 %copy-start.2 = (bf16[128,2048]{1,0:T(8,128)(2,1)S(1)}, bf16[128,2048]{1,0:T(8,128)(2,1)}, u32[]{:S(2)}) copy-start(bf16[128,2048]{1,0:T(8,128)(2,1)} %param.8) | copy-start | bytes 1572868
  136.3 13.4 %copy-start.6 = (bf16[384,768]{1,0:T(8,128)(2,1)S(1)}, bf16[384,768]{1,0:T(8,128)(2,1)}, u32[]{:S(2)}) copy-start(bf16[384,768]{1,0:T(8,128)(2,1)} %copy-done.5) | copy-start | bytes 1769476
  143.4 12.7 %all-to-all-start.4 = ((f32[16,128,16]{1,2,0:T(8,128)}), f32[16,128,16]{1,2,0:T(8,128)S(1)}, u32[]{:S(2)}, u32[]{:S(2)}) async-start(f32[16,128,16]{1,2,0:T(8,128)} %bitcast.76), calls=%async_computation.4 | async-start | bytes 262144 | tf_op jit(solution)/shard_map/all_to_all | solution.py:23
  156.1 30.7 %all-to-all-start.3 = ((bf16[16,24,2048]{2,1,0:T(8,128)(2,1)}), bf16[16,24,2048]{2,1,0:T(8,128)(2,1)S(1)}, u32[]{:S(2)}, u32[]{:S(2)}) async-start(bf16[16,24,2048]{2,1,0:T(8,128)(2,1)} %bitcast.85), calls=%async_computation.3 | async-start | bytes 3145728 | tf_op jit(solution)/shard_map/all_to_all | solution.py:158
  162.5 21.1 %copy-start.12 = (s32[16]{0:T(128)S(1)}, s32[16]{0:T(128)}, u32[]{:S(2)}) copy-start(s32[16]{0:T(128)} %param.11) | copy-start | bytes 196
  170.8 31.2 %collective-permute-start.4 = (bf16[3,128,768]{2,1,0:T(8,128)(2,1)}, bf16[3,128,768]{2,1,0:T(8,128)(2,1)}, u32[]{:S(2)}, u32[]{:S(2)}) collective-permute-start(bf16[3,128,768]{2,1,0:T(8,128)(2,1)} %pad_maximum_fusion.1), channel_id=1, source_target_pairs={{0,8},{1,9},{2,10},{3,11},{4,12},{5,13},{6,14},{7,15},{8,0},{9,1},... | collective-permute-start | bytes 1769480 | tf_op jit(solution)/shard_map/ppermute | solution.py:9
  172.8 30.9 %collective-permute-start.5 = (bf16[3,128,768]{2,1,0:T(8,128)(2,1)}, bf16[3,128,768]{2,1,0:T(8,128)(2,1)}, u32[]{:S(2)}, u32[]{:S(2)}) collective-permute-start(bf16[3,128,768]{2,1,0:T(8,128)(2,1)} %pad_maximum_fusion.1), channel_id=1, source_target_pairs={{0,4},{1,5},{2,6},{3,7},{4,0},{5,1},{6,2},{7,3},{8,12},{9,13},{10,... | collective-permute-start | bytes 1769480 | tf_op jit(solution)/shard_map/ppermute | solution.py:9
  174.3 29.4 %collective-permute-start.6 = (bf16[3,128,768]{2,1,0:T(8,128)(2,1)}, bf16[3,128,768]{2,1,0:T(8,128)(2,1)}, u32[]{:S(2)}, u32[]{:S(2)}) collective-permute-start(bf16[3,128,768]{2,1,0:T(8,128)(2,1)} %pad_maximum_fusion.1), channel_id=1, source_target_pairs={{0,2},{1,3},{2,0},{3,1},{4,6},{5,7},{6,4},{7,5},{8,10},{9,11},{10,... | collective-permute-start | bytes 1769480 | tf_op jit(solution)/shard_map/ppermute | solution.py:9
  177.1 28.0 %collective-permute-start.7 = (bf16[3,128,768]{2,1,0:T(8,128)(2,1)}, bf16[3,128,768]{2,1,0:T(8,128)(2,1)}, u32[]{:S(2)}, u32[]{:S(2)}) collective-permute-start(bf16[3,128,768]{2,1,0:T(8,128)(2,1)} %pad_maximum_fusion.1), channel_id=1, source_target_pairs={{0,1},{1,0},{2,3},{3,2},{4,5},{5,4},{6,7},{7,6},{8,9},{9,8},{10,11... | collective-permute-start | bytes 1769480 | tf_op jit(solution)/shard_map/ppermute | solution.py:9
  177.8 1.2 collective-permute-start
  178.9 3.7 %collective-permute-start.1 = (f32[128,16]{0,1:T(8,128)S(1)}, f32[128,16]{0,1:T(8,128)S(1)}, u32[]{:S(2)}, u32[]{:S(2)}) collective-permute-start(f32[128,16]{0,1:T(8,128)S(1)} %add.85), channel_id=1, source_target_pairs={{0,32},{16,48},{32,0},{48,16},{64,96},{80,112},{96,64},{112,80},{1... | collective-permute-start | bytes 24584 | tf_op jit(solution)/shard_map/ppermute | solution.py:9
  182.6 11.7 %collective-permute-start.2 = (f32[128,16]{0,1:T(8,128)S(1)}, f32[128,16]{0,1:T(8,128)S(1)}, u32[]{:S(2)}, u32[]{:S(2)}) collective-permute-start(f32[128,16]{0,1:T(8,128)S(1)} %add.86), channel_id=1, source_target_pairs={{0,64},{16,80},{32,96},{48,112},{64,0},{80,16},{96,32},{112,48},{1... | collective-permute-start | bytes 24584 | tf_op jit(solution)/shard_map/ppermute | solution.py:9
  194.3 7.6 %collective-permute-start.3 = (f32[128,16]{0,1:T(8,128)S(1)}, f32[128,16]{0,1:T(8,128)S(1)}, u32[]{:S(2)}, u32[]{:S(2)}) collective-permute-start(f32[128,16]{0,1:T(8,128)S(1)} %add.87), channel_id=1, source_target_pairs={{0,128},{16,144},{32,160},{48,176},{64,192},{80,208},{96,224},{112... | collective-permute-start | bytes 24584 | tf_op jit(solution)/shard_map/ppermute | solution.py:9
  205.8 13.8 %all-to-all-start.5 = ((f32[16,128,16]{1,2,0:T(8,128)}), f32[16,128,16]{1,2,0:T(8,128)S(1)}, u32[]{:S(2)}, u32[]{:S(2)}) async-start(f32[16,128,16]{1,2,0:T(8,128)} %broadcast_in_dim.19), calls=%async_computation.6 | async-start | bytes 262144 | tf_op jit(solution)/shard_map/all_to_all | solution.py:15
Sparse Core Ops, SparseCore 0:
  9.9 63.7 all-gather.1
  96.8 71.8 reduce-scatter.1

commit v5 on v3

--- a/solution.py
+++ b/solution.py
@@ -159,12 +159,13 @@
         d_rows.reshape(groups, capacity, width), "expert", split_axis=0, concat_axis=0, tiled=True
     ).reshape(total, width)
     d_expert = jnp.sum(d_returned[slot_index].astype(jnp.float32), axis=1)
+    joined = jnp.concatenate([d_pre_gate, d_pre_up], axis=1)
     pieces = [
-        row_major(contract_rows(slot_rows, jnp.concatenate([d_pre_gate, d_pre_up], axis=1))),
-        row_major(contract_rows(d_inbox, hidden_rows)),
+        row_major((contract_rows(slot_rows, joined) * grad_scale).astype(jnp.bfloat16)),
+        row_major((contract_rows(d_inbox, hidden_rows) * grad_scale).astype(jnp.bfloat16)),
     ]
     shares = lax.psum_scatter(
-        (jnp.concatenate(pieces, axis=1) * grad_scale).astype(jnp.bfloat16),
+        jnp.concatenate(pieces, axis=1),
         "dp",
         scatter_dimension=0,
         tiled=True,

time: 227 us -> 230 us (1.013)
  matrix products: 34.8 us -> 39.2 us
  local copies, waits for them, and re-layouts: 26.8 us -> 24.1 us
    convert_element_type x1 -> x0, other arithmetic: 4.85 us -> none  [on_device(): (jnp.concatenate(pieces, axis=1) * grad_scale).astype(jnp.bfloat16)]
    concatenate x0 -> x1, other arithmetic: none -> 4.53 us  [on_device(): jnp.concatenate(pieces, axis=1)]
    all_to_all x1, waiting for transfers between devices: 10 us -> 12.8 us  [on_device(): lax.all_to_all(outbox, 'expert', split_axis=0, concat_axis=0, tiled=True)]
    mul x2, local copies, waits for them, and re-layouts: 6.13 us -> 3.49 us  [on_device(): d_out = (gate_vals[:, :, None] * cot_wide[:, None, :]).astype(jnp.bfloat16)]
where the time goes in v5:
time: 230 us; the launch traced here: 229 us
  waiting for transfers between devices  72.7 us (32%)
  starting transfers between devices  50.1 us (22%)
  matrix products  39.2 us (17%)
  other arithmetic  25.7 us (11%)
  local copies, waits for them, and re-layouts  24.1 us (10%)
  between operations  16.9 us (7%)
    all_gather x1, waiting for transfers between devices, on_device(): gathered = lax.all_gather(held, 'dp', axis=1, tiled=True)  21.9 us
    all_to_all x1, waiting for transfers between devices, on_device(): lax.all_to_all(result, 'expert', split_axis=0, concat_axis=0, tiled=True)  15 us
    all_to_all x1, waiting for transfers between devices, on_device(): lax.all_to_all(outbox, 'expert', split_axis=0, concat_axis=0, tiled=True)  12.8 us
    ppermute x8, waiting for transfers between devices, swapped(): lax.ppermute(array, axis, [(i, i ^ 1 << stride) for i in range(lax.axis_s...  11.9 us
    ppermute x8, starting transfers between devices, swapped(): lax.ppermute(array, axis, [(i, i ^ 1 << stride) for i in range(lax.axis_s...  10.9 us
    all_to_all x1, starting transfers between devices, on_device(): lax.all_to_all(outbox, 'expert', split_axis=0, concat_axis=0, tiled=True)  7.48 us
    dot_general x3, matrix products, contract_rows(): lax.dot_general(left, right, (((0,), (0,)), ((), ())), preferred_element_...  7.29 us
    all_to_all x1, starting transfers between devices, on_device(): lax.all_to_all(result, 'expert', split_axis=0, concat_axis=0, tiled=True)  7.27 us
  transfers between devices with their start and end apart: 16, of which 11 were waited for; matrix products, arithmetic and copies ran while one was open for 30% of the time, Pallas kernels for 0%

profile of v5, /device:TPU:2, one launch (start us, length us, event | category | flops | bytes accessed | tf_op | source)
XLA Modules:
  0.0 228.8 jit_solution(15800149076690125286)
XLA Ops:
  12.7 3.5 %scatter_custom_fusion = bf16[384,2048]{1,0:T(8,128)(2,1)} fusion(s32[256]{0:T(256)S(1)} %bitcast.84, bf16[256,2048]{1,0:T(8,128)(2,1)S(1)} %reshape.199, bf16[]{:T(256)} %constant.16.clone.1), kind=kCustom, calls=%fused_computation.37 | custom fusion | bytes 1572866 | tf_op jit(solution)/shard_map/scatter | solution.py:57
  16.2 7.5 %all-to-all-start = ((bf16[16,24,2048]{2,1,0:T(8,128)(2,1)}), bf16[16,24,2048]{2,1,0:T(8,128)(2,1)}, u32[]{:S(2)}, u32[]{:S(2)}) async-start(bf16[16,24,2048]{2,1,0:T(8,128)(2,1)} %bitcast.3), calls=%async_computation | async-start | bytes 3145728 | tf_op jit(solution)/shard_map/all_to_all | solution.py:122
  24.7 2.4 %mul.162 = f32[256,2048]{1,0:T(8,128)} reshape(f32[128,2,2048]{2,1,0:T(2,128)S(1)} %mul.161) | data formatting | bytes 4194304 | tf_op jit(solution)/shard_map/mul | solution.py:142
  27.7 4.6 %scatter_custom_fusion.1 = bf16[384,2048]{1,0:T(8,128)(2,1)} fusion(s32[256]{0:T(256)S(1)} %bitcast.85, f32[256,2048]{1,0:T(8,128)} %mul.162, f32[256]{0:T(256)S(1)} %div.42, bf16[]{:T(256)} %constant.16.clone.1), kind=kCustom, calls=%fused_computation.34 | custom fusion | flops 1048576 | bytes 3671042 | tf_op jit(solution)/shard_map/scatter | solution.py:57
  32.3 12.8 %all-to-all-done = bf16[16,24,2048]{2,1,0:T(8,128)(2,1)} async-done(((bf16[16,24,2048]{2,1,0:T(8,128)(2,1)}), bf16[16,24,2048]{2,1,0:T(8,128)(2,1)}, u32[]{:S(2)}, u32[]{:S(2)}) %all-to-all-start) | async-done | bytes 1572896 | tf_op jit(solution)/shard_map/all_to_all | solution.py:122
  45.1 6.3 %all-to-all-start.2 = ((bf16[16,24,2048]{2,1,0:T(8,128)(2,1)}), bf16[16,24,2048]{2,1,0:T(8,128)(2,1)S(1)}, u32[]{:S(2)}, u32[]{:S(2)}) async-start(bf16[16,24,2048]{2,1,0:T(8,128)(2,1)} %bitcast.11), calls=%async_computation.2 | async-start | bytes 3145728 | tf_op jit(solution)/shard_map/all_to_all | solution.py:144
  51.7 21.9 %all-gather.2.cloned.1.call-done = bf16[3,2048,768]{2,1,0:T(8,128)(2,1)} async-done(((bf16[3,128,768]{2,1,0:T(8,128)(2,1)}), bf16[3,2048,768]{2,1,0:T(8,128)(2,1)}) %all-gather.2.cloned.1.call-update) | async-done | bytes 9437200 | tf_op jit(solution)/shard_map/all_gather | solution.py:117
  73.6 4.7 %fusion.1 = f32[384,768]{1,0:T(8,128)} fusion(bf16[384,2048]{1,0:T(8,128)(2,1)} %bitcast.4, bf16[3,2048,768]{2,1,0:T(8,128)(2,1)} %all-gather.2.cloned.1.call-done), kind=kOutput, calls=%fused_computation.13 | convolution fusion | flops 1207959552 | bytes 5898240 | tf_op jit(solution)/shard_map/dot_general | solution.py:61
  78.4 4.8 %fusion.2 = f32[384,768]{1,0:T(8,128)} fusion(bf16[384,2048]{1,0:T(8,128)(2,1)} %bitcast.4, bf16[3,2048,768]{2,1,0:T(8,128)(2,1)} %all-gather.2.cloned.1.call-done), kind=kOutput, calls=%fused_computation.14 | convolution fusion | flops 1207959552 | bytes 5898240 | tf_op jit(solution)/shard_map/dot_general | solution.py:62
  83.1 4.2 %multiply_convert_fusion.3 = (bf16[384,768]{1,0:T(8,128)(2,1)S(1)}, bf16[384,768]{1,0:T(8,128)(2,1)S(1)}, bf16[384,768]{1,0:T(8,128)(2,1)S(1)}) fusion(f32[384,768]{1,0:T(8,128)} %fusion.1, f32[384,768]{1,0:T(8,128)} %fusion.2, bf16[384,2048]{1,0:T(8,128)(2,1)S(1)} %bitcast.80, bf16[3,2048,768]{2,1,0:T(8,128)(2,1)} %all-gather.2.cloned.1.call-done), kind=kOutput, calls=%fused_computation.25 | convolution fusion | flops 1212678144 | bytes 8847360 | tf_op jit(solution)/shard_map/dot_general | solution.py:71
  89.3 5.3 %multiply_convert_fusion = bf16[2048,1536]{1,0:T(8,128)(2,1)S(1)} fusion(bf16[384,2048]{1,0:T(8,128)(2,1)} %bitcast.4, bf16[384,768]{1,0:T(8,128)(2,1)S(1)} %get-tuple-element.24, bf16[384,768]{1,0:T(8,128)(2,1)S(1)} %get-tuple-element.25), kind=kOutput, calls=%fused_computation.4 | convolution fusion | flops 2424569856 | bytes 9043968 | tf_op jit(solution)/shard_map/dot_general | solution.py:88
  94.6 4.5 %pad_maximum_fusion = bf16[2048,2304]{1,0:T(8,128)(2,1)} fusion(bf16[2048,768]{1,0:T(8,128)(2,1)S(1)} %multiply_convert_fusion.1, bf16[2048,1536]{1,0:T(8,128)(2,1)S(1)} %multiply_convert_fusion), kind=kLoop, calls=%fused_computation.5 | loop fusion | flops 18874368 | bytes 18874368 | tf_op jit(solution)/shard_map/concatenate | solution.py:168
  100.2 4.5 %convolution_convert_fusion = bf16[384,2048]{1,0:T(8,128)(2,1)} fusion(bf16[384,768]{1,0:T(8,128)(2,1)S(1)} %copy-done.8, bf16[3,2048,768]{2,1,0:T(8,128)(2,1)} %all-gather.2.cloned.1.call-done), kind=kOutput, calls=%fused_computation.11 | convolution fusion | flops 1208745984 | bytes 5308416 | tf_op jit(solution)/shard_map/dot_general | solution.py:64
  104.7 7.3 %all-to-all-start.1 = ((bf16[16,24,2048]{2,1,0:T(8,128)(2,1)}), bf16[16,24,2048]{2,1,0:T(8,128)(2,1)S(1)}, u32[]{:S(2)}, u32[]{:S(2)}) async-start(bf16[16,24,2048]{2,1,0:T(8,128)(2,1)} %bitcast.82), calls=%async_computation.1 | async-start | bytes 3145728 | tf_op jit(solution)/shard_map/all_to_all | solution.py:135
  113.5 5.2 %fusion = f32[384,2048]{1,0:T(8,128)} fusion(bf16[384,768]{1,0:T(8,128)(2,1)} %copy-done.6, bf16[3,2048,768]{2,1,0:T(8,128)(2,1)} %all-gather.2.cloned.1.call-done), kind=kOutput, calls=%fused_computation.12 | convolution fusion | flops 1207959552 | bytes 6881280 | tf_op jit(solution)/shard_map/dot_general | solution.py:76
  118.8 15.0 %all-to-all-done.1 = bf16[16,24,2048]{2,1,0:T(8,128)(2,1)S(1)} async-done(((bf16[16,24,2048]{2,1,0:T(8,128)(2,1)}), bf16[16,24,2048]{2,1,0:T(8,128)(2,1)S(1)}, u32[]{:S(2)}, u32[]{:S(2)}) %all-to-all-start.1) | async-done | bytes 1572896 | tf_op jit(solution)/shard_map/all_to_all | solution.py:135
  133.8 2.4 %gather_fusion = bf16[256,2048]{1,0:T(8,128)(2,1)} fusion(bf16[384,2048]{1,0:T(8,128)(2,1)S(1)} %bitcast.78, s32[1024]{0:T(1024)S(1)} %pad_clamp_fusion), kind=kCustom, calls=%fused_computation | custom fusion | bytes 2098176 | tf_op jit(solution)/shard_map/gather | solution.py:138
  136.2 2.4 %reshape.213 = f32[128,2,2048]{2,1,0:T(2,128)S(1)} reshape(bf16[256,2048]{1,0:T(8,128)(2,1)} %gather_fusion) | data formatting | bytes 3145728 | tf_op jit(solution)/shard_map/convert_element_type | solution.py:138
  138.5 6.1 %multiply_reduce_fusion = (f32[128,2]{1,0:T(8,128)S(1)}, bf16[128,2048]{1,0:T(8,128)(2,1)}) fusion(f32[128,2,2048]{2,1,0:T(2,128)S(1)} %reshape.213, f32[128,2048]{1,0:T(8,128)} %convert_element_type.57, f32[128,2]{1,0:T(8,128)S(1)} %copy.38), kind=kLoop, calls=%fused_computation.19 | loop fusion | flops 1834752 | bytes 3672064 | tf_op jit(solution)/shard_map/reduce_sum | solution.py:141
  145.6 6.3 %all-to-all-start.4 = ((f32[16,128,16]{1,2,0:T(8,128)}), f32[16,128,16]{1,2,0:T(8,128)S(1)}, u32[]{:S(2)}, u32[]{:S(2)}) async-start(f32[16,128,16]{1,2,0:T(8,128)} %bitcast.76), calls=%async_computation.4 | async-start | bytes 262144 | tf_op jit(solution)/shard_map/all_to_all | solution.py:23
  152.0 5.8 %add_convert_fusion = bf16[384,2048]{1,0:T(8,128)(2,1)} fusion(f32[384,2048]{1,0:T(8,128)} %fusion, bf16[384,768]{1,0:T(8,128)(2,1)} %copy-done.5, bf16[3,2048,768]{2,1,0:T(8,128)(2,1)} %all-gather.2.cloned.1.call-done), kind=kOutput, calls=%fused_computation.10 | convolution fusion | flops 1209532416 | bytes 8454144 | tf_op jit(solution)/shard_map/dot_general | solution.py:77
  158.4 6.7 %all-to-all-start.3 = ((bf16[16,24,2048]{2,1,0:T(8,128)(2,1)}), bf16[16,24,2048]{2,1,0:T(8,128)(2,1)S(1)}, u32[]{:S(2)}, u32[]{:S(2)}) async-start(bf16[16,24,2048]{2,1,0:T(8,128)(2,1)} %bitcast.79), calls=%async_computation.3 | async-start | bytes 3145728 | tf_op jit(solution)/shard_map/all_to_all | solution.py:158
  165.1 6.0 %reduce-scatter.2.cloned.1.call-done = bf16[128,2304]{1,0:T(8,128)(2,1)} async-done(((bf16[2048,2304]{1,0:T(8,128)(2,1)}), bf16[128,2304]{1,0:T(8,128)(2,1)}) %reduce-scatter.2.cloned.1.call-update) | async-done | bytes 589840 | tf_op jit(solution)/shard_map/reduce_scatter | solution.py:167
  174.0 2.7 %collective-permute-start.5 = (bf16[3,128,768]{2,1,0:T(8,128)(2,1)S(1)}, bf16[3,128,768]{2,1,0:T(8,128)(2,1)}, u32[]{:S(2)}, u32[]{:S(2)}) collective-permute-start(bf16[3,128,768]{2,1,0:T(8,128)(2,1)S(1)} %pad_maximum_fusion.2), channel_id=1, source_target_pairs={{0,2},{1,3},{2,0},{3,1},{4,6},{5,7},{6,4},{7,5},{8,10},{9,11},{10,... | collective-permute-start | bytes 1769480 | tf_op jit(solution)/shard_map/ppermute | solution.py:9
  180.5 3.6 %collective-permute-done.1 = f32[128,16]{0,1:T(8,128)S(1)} collective-permute-done((f32[128,16]{0,1:T(8,128)S(1)}, f32[128,16]{0,1:T(8,128)S(1)}, u32[]{:S(2)}, u32[]{:S(2)}) %collective-permute-start.1) | collective-permute-done | bytes 8224 | tf_op jit(solution)/shard_map/ppermute | solution.py:9
  190.8 2.4 %reshape.214 = f32[128,2,2048]{2,1,0:T(2,128)S(1)} reshape(bf16[256,2048]{1,0:T(8,128)(2,1)} %gather_fusion.1) | data formatting | bytes 3145728 | tf_op jit(solution)/shard_map/convert_element_type | solution.py:161
  193.2 3.9 %reduce_sum.118 = f32[128,2048]{1,0:T(8,128)} reduce(f32[128,2,2048]{2,1,0:T(2,128)S(1)} %reshape.214, f32[]{:T(128)} %constant.15.clone.1), dimensions={1}, to_apply=%region_9.10 | reduce | flops 262144 | bytes 3145732 | tf_op jit(solution)/shard_map/reduce_sum | solution.py:161
  197.1 2.9 %collective-permute-start.3 = (f32[128,16]{0,1:T(8,128)S(1)}, f32[128,16]{0,1:T(8,128)S(1)}, u32[]{:S(2)}, u32[]{:S(2)}) collective-permute-start(f32[128,16]{0,1:T(8,128)S(1)} %add.87), channel_id=1, source_target_pairs={{0,128},{16,144},{32,160},{48,176},{64,192},{80,208},{96,224},{112... | collective-permute-start | bytes 24584 | tf_op jit(solution)/shard_map/ppermute | solution.py:9
  202.3 2.4 %collective-permute-done.3 = f32[128,16]{0,1:T(8,128)S(1)} collective-permute-done((f32[128,16]{0,1:T(8,128)S(1)}, f32[128,16]{0,1:T(8,128)S(1)}, u32[]{:S(2)}, u32[]{:S(2)}) %collective-permute-start.3) | collective-permute-done | bytes 8224 | tf_op jit(solution)/shard_map/ppermute | solution.py:9
  204.7 4.1 %collective-permute-done.5 = bf16[3,128,768]{2,1,0:T(8,128)(2,1)} collective-permute-done((bf16[3,128,768]{2,1,0:T(8,128)(2,1)S(1)}, bf16[3,128,768]{2,1,0:T(8,128)(2,1)}, u32[]{:S(2)}, u32[]{:S(2)}) %collective-permute-start.5) | collective-permute-done | bytes 589856 | tf_op jit(solution)/shard_map/ppermute | solution.py:9
  210.1 4.8 %all-to-all-start.5 = ((f32[16,128,16]{1,2,0:T(8,128)}), f32[16,128,16]{1,2,0:T(8,128)S(1)}, u32[]{:S(2)}, u32[]{:S(2)}) async-start(f32[16,128,16]{1,2,0:T(8,128)} %broadcast_in_dim.19), calls=%async_computation.6 | async-start | bytes 262144 | tf_op jit(solution)/shard_map/all_to_all | solution.py:15
  217.0 4.4 %all-to-all-done.5 = f32[16,128,16]{1,2,0:T(8,128)S(1)} async-done(((f32[16,128,16]{1,2,0:T(8,128)}), f32[16,128,16]{1,2,0:T(8,128)S(1)}, u32[]{:S(2)}, u32[]{:S(2)}) %all-to-all-start.5) | async-done | bytes 131104 | tf_op jit(solution)/shard_map/all_to_all | solution.py:15
  (90 shorter events, 30.5 us)
Async XLA Ops:
  7.2 20.0 %copy-start = (bf16[2048,16]{0,1:T(8,128)(2,1)S(1)}, bf16[2048,16]{0,1:T(8,128)(2,1)}, u32[]{:S(2)}) copy-start(bf16[2048,16]{0,1:T(8,128)(2,1)} %param.12) | copy-start | bytes 196612
  7.2 4.4 %copy-start.1 = (bf16[128,2048]{1,0:T(8,128)(2,1)S(1)}, bf16[128,2048]{1,0:T(8,128)(2,1)}, u32[]{:S(2)}) copy-start(bf16[128,2048]{1,0:T(8,128)(2,1)} %param.8) | copy-start | bytes 1572868
  7.2 66.4 %all-gather.2.cloned.1.call-start = ((), (), s32[]{:S(2)}) async-start(), calls=%async_computation.7 | async-start | bytes 10027008 | tf_op jit(solution)/shard_map/all_gather | solution.py:117
  12.7 10.9 %copy-start.2 = (bf16[128,2048]{1,0:T(8,128)(2,1)S(1)}, bf16[128,2048]{1,0:T(8,128)(2,1)}, u32[]{:S(2)}) copy-start(bf16[128,2048]{1,0:T(8,128)(2,1)} %param.9) | copy-start | bytes 1572868
  16.2 29.0 %all-to-all-start = ((bf16[16,24,2048]{2,1,0:T(8,128)(2,1)}), bf16[16,24,2048]{2,1,0:T(8,128)(2,1)}, u32[]{:S(2)}, u32[]{:S(2)}) async-start(bf16[16,24,2048]{2,1,0:T(8,128)(2,1)} %bitcast.3), calls=%async_computation | async-start | bytes 3145728 | tf_op jit(solution)/shard_map/all_to_all | solution.py:122
  24.7 2.7 %copy-start.3 = (s32[128,2]{0,1:T(2,128)S(1)}, s32[128,2]{0,1:T(2,128)}, u32[]{:S(2)}) copy-start(s32[128,2]{0,1:T(2,128)} %param.10) | copy-start | bytes 3076
  45.1 38.0 %all-to-all-start.2 = ((bf16[16,24,2048]{2,1,0:T(8,128)(2,1)}), bf16[16,24,2048]{2,1,0:T(8,128)(2,1)S(1)}, u32[]{:S(2)}, u32[]{:S(2)}) async-start(bf16[16,24,2048]{2,1,0:T(8,128)(2,1)} %bitcast.11), calls=%async_computation.2 | async-start | bytes 3145728 | tf_op jit(solution)/shard_map/all_to_all | solution.py:144
  51.4 119.6 %reduce-scatter.2.cloned.1.call-start = ((), (), s32[]{:S(2)}) async-start(), calls=%async_computation.8 | async-start | bytes 10027008 | tf_op jit(solution)/shard_map/reduce_scatter | solution.py:167
  87.4 1.9 copy-start.7
  87.4 1.9 copy-start.5
  87.4 1.9 copy-start.6
  99.1 1.1 copy-start.8
  104.7 29.1 %all-to-all-start.1 = ((bf16[16,24,2048]{2,1,0:T(8,128)(2,1)}), bf16[16,24,2048]{2,1,0:T(8,128)(2,1)S(1)}, u32[]{:S(2)}, u32[]{:S(2)}) async-start(bf16[16,24,2048]{2,1,0:T(8,128)(2,1)} %bitcast.82), calls=%async_computation.1 | async-start | bytes 3145728 | tf_op jit(solution)/shard_map/all_to_all | solution.py:135
  145.6 12.7 %all-to-all-start.4 = ((f32[16,128,16]{1,2,0:T(8,128)}), f32[16,128,16]{1,2,0:T(8,128)S(1)}, u32[]{:S(2)}, u32[]{:S(2)}) async-start(f32[16,128,16]{1,2,0:T(8,128)} %bitcast.76), calls=%async_computation.4 | async-start | bytes 262144 | tf_op jit(solution)/shard_map/all_to_all | solution.py:23
  158.4 26.9 %copy-start.4 = (s32[16]{0:T(128)S(1)}, s32[16]{0:T(128)}, u32[]{:S(2)}) copy-start(s32[16]{0:T(128)} %param.11) | copy-start | bytes 196
  158.4 30.1 %all-to-all-start.3 = ((bf16[16,24,2048]{2,1,0:T(8,128)(2,1)}), bf16[16,24,2048]{2,1,0:T(8,128)(2,1)S(1)}, u32[]{:S(2)}, u32[]{:S(2)}) async-start(bf16[16,24,2048]{2,1,0:T(8,128)(2,1)} %bitcast.79), calls=%async_computation.3 | async-start | bytes 3145728 | tf_op jit(solution)/shard_map/all_to_all | solution.py:158
  172.3 32.4 %collective-permute-start.4 = (bf16[3,128,768]{2,1,0:T(8,128)(2,1)S(1)}, bf16[3,128,768]{2,1,0:T(8,128)(2,1)}, u32[]{:S(2)}, u32[]{:S(2)}) collective-permute-start(bf16[3,128,768]{2,1,0:T(8,128)(2,1)S(1)} %pad_maximum_fusion.2), channel_id=1, source_target_pairs={{0,1},{1,0},{2,3},{3,2},{4,5},{5,4},{6,7},{7,6},{8,9},{9,8},{10,11... | collective-permute-start | bytes 1769480 | tf_op jit(solution)/shard_map/ppermute | solution.py:9
  174.0 34.8 %collective-permute-start.5 = (bf16[3,128,768]{2,1,0:T(8,128)(2,1)S(1)}, bf16[3,128,768]{2,1,0:T(8,128)(2,1)}, u32[]{:S(2)}, u32[]{:S(2)}) collective-permute-start(bf16[3,128,768]{2,1,0:T(8,128)(2,1)S(1)} %pad_maximum_fusion.2), channel_id=1, source_target_pairs={{0,2},{1,3},{2,0},{3,1},{4,6},{5,7},{6,4},{7,5},{8,10},{9,11},{10,... | collective-permute-start | bytes 1769480 | tf_op jit(solution)/shard_map/ppermute | solution.py:9
  176.6 32.2 %collective-permute-start.6 = (bf16[3,128,768]{2,1,0:T(8,128)(2,1)S(1)}, bf16[3,128,768]{2,1,0:T(8,128)(2,1)}, u32[]{:S(2)}, u32[]{:S(2)}) collective-permute-start(bf16[3,128,768]{2,1,0:T(8,128)(2,1)S(1)} %pad_maximum_fusion.2), channel_id=1, source_target_pairs={{0,4},{1,5},{2,6},{3,7},{4,0},{5,1},{6,2},{7,3},{8,12},{9,13},{10,... | collective-permute-start | bytes 1769480 | tf_op jit(solution)/shard_map/ppermute | solution.py:9
  177.3 32.1 %collective-permute-start.7 = (bf16[3,128,768]{2,1,0:T(8,128)(2,1)S(1)}, bf16[3,128,768]{2,1,0:T(8,128)(2,1)}, u32[]{:S(2)}, u32[]{:S(2)}) collective-permute-start(bf16[3,128,768]{2,1,0:T(8,128)(2,1)S(1)} %pad_maximum_fusion.2), channel_id=1, source_target_pairs={{0,8},{1,9},{2,10},{3,11},{4,12},{5,13},{6,14},{7,15},{8,0},{9,1},... | collective-permute-start | bytes 1769480 | tf_op jit(solution)/shard_map/ppermute | solution.py:9
  179.4 1.2 collective-permute-start
  180.5 3.7 %collective-permute-start.1 = (f32[128,16]{0,1:T(8,128)S(1)}, f32[128,16]{0,1:T(8,128)S(1)}, u32[]{:S(2)}, u32[]{:S(2)}) collective-permute-start(f32[128,16]{0,1:T(8,128)S(1)} %add.85), channel_id=1, source_target_pairs={{0,32},{16,48},{32,0},{48,16},{64,96},{80,112},{96,64},{112,80},{1... | collective-permute-start | bytes 24584 | tf_op jit(solution)/shard_map/ppermute | solution.py:9
  184.2 12.9 %collective-permute-start.2 = (f32[128,16]{0,1:T(8,128)S(1)}, f32[128,16]{0,1:T(8,128)S(1)}, u32[]{:S(2)}, u32[]{:S(2)}) collective-permute-start(f32[128,16]{0,1:T(8,128)S(1)} %add.86), channel_id=1, source_target_pairs={{0,64},{16,80},{32,96},{48,112},{64,0},{80,16},{96,32},{112,48},{1... | collective-permute-start | bytes 24584 | tf_op jit(solution)/shard_map/ppermute | solution.py:9
  197.1 7.6 %collective-permute-start.3 = (f32[128,16]{0,1:T(8,128)S(1)}, f32[128,16]{0,1:T(8,128)S(1)}, u32[]{:S(2)}, u32[]{:S(2)}) collective-permute-start(f32[128,16]{0,1:T(8,128)S(1)} %add.87), channel_id=1, source_target_pairs={{0,128},{16,144},{32,160},{48,176},{64,192},{80,208},{96,224},{112... | collective-permute-start | bytes 24584 | tf_op jit(solution)/shard_map/ppermute | solution.py:9
  210.1 11.2 %all-to-all-start.5 = ((f32[16,128,16]{1,2,0:T(8,128)}), f32[16,128,16]{1,2,0:T(8,128)S(1)}, u32[]{:S(2)}, u32[]{:S(2)}) async-start(f32[16,128,16]{1,2,0:T(8,128)} %broadcast_in_dim.19), calls=%async_computation.6 | async-start | bytes 262144 | tf_op jit(solution)/shard_map/all_to_all | solution.py:15
Sparse Core Ops, SparseCore 0:
  9.8 63.7 all-gather.1
  99.2 71.8 reduce-scatter.1
